TPU v7x, 128 devices: a whole 4x4x4 slice. The times are simulated.
128 devices in a mesh: rows: 32 (over y, z, x_lo), chan: 4 (over x_hi, core).
Axes of the slice: x: 4 (x_hi: 2, x_lo: 2; x = x_hi * 2 + x_lo), y: 4, z: 4, core: 2. Of those that a mesh axis runs over, the one named last changes fastest.
Arguments:
- latent: bfloat16 [128, 128, 1280], P('rows', None, 'chan'), may hold values from -6 to 6
- stale_latent: bfloat16 [64, 128, 1280], P('rows', None, 'chan'), may hold values from -6 to 6
- stale_hidden: bfloat16 [64, 128, 1280], P('rows', None, 'chan'), may hold values from -4 to 4
- first_kernel: bfloat16 [3, 3, 1280, 1280], P(None, None, None, 'chan'), may hold values from -0.0546875 to 0.0546875
- second_kernel: bfloat16 [3, 3, 1280, 1280], P(None, None, None, 'chan'), may hold values from -0.0546875 to 0.0546875
- scale_table: float32 [1000, 1280], P(None, 'chan'), may hold values from 0.3 to 3
- timestep: int32 [1], replicated, may hold values from 0 to 999
- cotangent: bfloat16 [128, 128, 1280], P('rows', None, 'chan'), may hold values from -6 to 6
Outputs:
- output: bfloat16 [128, 128, 1280], P('rows', None, 'chan')
- grad_latent: bfloat16 [128, 128, 1280], P('rows', None, 'chan')
- grad_first: float32 [3, 3, 1280, 1280], P(None, None, 'rows', 'chan')
- grad_second: float32 [3, 3, 1280, 1280], P(None, None, 'rows', 'chan')
Inputs may be any that keep to these rules, and one draw needn't show every extreme that they name: `timestep`: selects a row of scale_table.
All inputs are finite; a program needn't handle non-finite values.
Results may differ from a plain program's by a relative error of at most 0.0058.
Values may be sent and summed in bfloat16 or wider, within the bound.
No kernel may reach another device: no remote copies, remote signals or barrier semaphores. Data moves between devices by JAX's collectives and lax.ppermute only.
A program may use at most 192 MiB of HBM per device.

v0:
```python
import jax
import jax.numpy as jnp
from jax import lax
from jax.sharding import PartitionSpec as P


def extended(shard, sides, width):
    for axis, dim in sides:
        peers, length = (lax.axis_size(axis), shard.shape[dim])
        up = [(i, (i + 1) % peers) for i in range(peers - 1)]
        down = [(j, i) for i, j in up]
        last = lax.slice_in_dim(shard, length - width, length, axis=dim)
        leading = lax.slice_in_dim(shard, 0, width, axis=dim)
        before = lax.ppermute(last, axis, up)
        after = lax.ppermute(leading, axis, down)
        shard = jnp.concatenate([before, shard, after], axis=dim)
    return shard


def silu_slope(values):
    logistic = jax.nn.sigmoid(values)
    return logistic * (1.0 + values * (1.0 - logistic))


def conv_rows(padded, kernel):
    result = lax.conv_general_dilated(
        padded[None],
        kernel,
        (1, 1),
        ((0, 0), (1, 1)),
        dimension_numbers=("NHWC", "HWIO", "NHWC"),
        preferred_element_type=jnp.float32,
    )
    return result[0]


def flipped(kernel):
    return jnp.transpose(kernel[::-1, ::-1], (0, 1, 3, 2))


def tap_sums(padded, grads):
    row_count, col_count, out_width = grads.shape
    flat_grads = grads.reshape(row_count * col_count, out_width)
    pieces = []
    for row_tap in range(3):
        for col_tap in range(3):
            window = padded[row_tap : row_tap + row_count, col_tap : col_tap + col_count]
            window = window.reshape(row_count * col_count, -1)
            pieces.append(
                lax.dot_general(
                    window, flat_grads, (((0,), (0,)), ((), ())), preferred_element_type=jnp.float32
                )
            )
    stacked = jnp.stack(pieces)
    return stacked.reshape(3, 3, stacked.shape[1], out_width)


def on_device(
    latent,
    stale_latent,
    stale_hidden,
    first_kernel,
    second_kernel,
    scale_table,
    timestep,
    cotangent,
):
    row_index = lax.axis_index("rows")
    row_devices = lax.axis_size("rows")
    height = latent.shape[0] * row_devices
    latent_f = latent.astype(jnp.float32)
    act = jax.nn.silu(latent_f).astype(jnp.bfloat16)
    edge_act = jax.nn.silu(stale_latent.astype(jnp.float32)).astype(jnp.bfloat16)
    act_all, edge_all = (
        lax.all_gather(act, "chan", axis=2, tiled=True),
        lax.all_gather(edge_act, "chan", axis=2, tiled=True),
    )

    def stale_pad(field, edges):
        above = jnp.where(row_index > 0, edges[0], jnp.zeros_like(edges[0]))
        below = jnp.where(row_index < row_devices - 1, edges[1], jnp.zeros_like(edges[1]))
        return jnp.concatenate([above[None], field, below[None]], axis=0)

    pre_act = conv_rows(stale_pad(act_all, edge_all), first_kernel)
    steps_iota = jnp.arange(scale_table.shape[0])[:, None]
    step_scale = jnp.sum(jnp.where(steps_iota == timestep[0], scale_table, 0.0), axis=0)
    scaled = pre_act * step_scale
    hidden = jax.nn.silu(scaled).astype(jnp.bfloat16)
    hidden_all, edge_hidden = (
        lax.all_gather(hidden, "chan", axis=2, tiled=True),
        lax.all_gather(stale_hidden, "chan", axis=2, tiled=True),
    )
    output = (latent_f + conv_rows(stale_pad(hidden_all, edge_hidden), second_kernel)).astype(
        jnp.bfloat16
    )
    grad_pad = extended(cotangent, (("rows", 0),), 1)
    grad_hidden = lax.psum_scatter(
        conv_rows(grad_pad, flipped(second_kernel)), "chan", scatter_dimension=2, tiled=True
    )
    delta = (grad_hidden * silu_slope(scaled) * step_scale).astype(jnp.bfloat16)
    delta_pad = extended(delta, (("rows", 0),), 1)
    grad_pre = lax.psum_scatter(
        conv_rows(delta_pad, flipped(first_kernel)), "chan", scatter_dimension=2, tiled=True
    )
    grad_latent = (
        latent_f * 0.0 + cotangent.astype(jnp.float32) + grad_pre * silu_slope(latent_f)
    ).astype(jnp.bfloat16)
    rim_fields = extended(jnp.stack((act_all, hidden_all)), (("rows", 1),), 1)
    rim_fields = jnp.pad(rim_fields, ((0, 0), (0, 0), (1, 1), (0, 0)))
    grad_second = (
        lax.psum_scatter(
            tap_sums(rim_fields[1], cotangent), "rows", scatter_dimension=2, tiled=True
        )
        / height
    )
    grad_first = (
        lax.psum_scatter(tap_sums(rim_fields[0], delta), "rows", scatter_dimension=2, tiled=True)
        / height
    )
    return (output, grad_latent, grad_first, grad_second)


def solution(mesh):
    in_specs = (
        P("rows", None, "chan"),
        P("rows", None, "chan"),
        P("rows", None, "chan"),
        P(None, None, None, "chan"),
        P(None, None, None, "chan"),
        P(None, "chan"),
        P(),
        P("rows", None, "chan"),
    )
    out_specs = (
        P("rows", None, "chan"),
        P("rows", None, "chan"),
        P(None, None, "rows", "chan"),
        P(None, None, "rows", "chan"),
    )
    return jax.shard_map(
        on_device, mesh=mesh, in_specs=in_specs, out_specs=out_specs, check_vma=False
    )
```

profile of v0, /device:TPU:8, one launch (start us, length us, event | category | flops | bytes accessed | tf_op | source)
XLA Modules:
  0.0 1016.7 jit_solution(12627822969924817040)
XLA Ops:
  8.2 6.8 collective-permute-start.1
  19.1 5.2 collective-permute-done
  26.2 7.6 convolution_select_fusion.1
  35.0 2.8 copy.122
  41.1 9.4 all_gather.13
  50.5 2.3 broadcast_select_fusion.2
  52.8 3.4 maximum_bitcast_fusion
  56.3 3.2 copy.136
  59.5 3.3 pad.5.clone
  62.8 2.7 reshape.18
  66.0 9.1 fusion.61
  76.6 37.0 %all-reduce.6.cloned.1.call-done = f32[4,128,1280]{1,0,2:T(4,128)} async-done(((f32[4,128,1280]{1,0,2:T(4,128)}), f32[4,128,1280]{1,0,2:T(4,128)}) %all-reduce.6.cloned.1.call-update) | async-done | bytes 2621456
  117.3 4.8 collective-permute-start.3
  122.1 2.4 collective-permute-start.2
  126.2 5.4 collective-permute-done.2
  134.6 7.6 convolution_select_fusion
  142.2 2.6 copy.127
  144.8 2.6 copy.131
  150.7 3.9 collective-permute-start.4
  156.3 4.4 copy.128
  160.9 7.6 collective-permute-done.5
  168.6 21.4 %collective-permute-done.4 = bf16[2,1,128,1280]{3,2,1,0:T(8,128)(2,1)} collective-permute-done((bf16[2,1,128,1280]{3,2,1,0:T(8,128)(2,1)}, bf16[2,1,128,1280]{3,2,1,0:T(8,128)(2,1)}, u32[]{:S(2)}, u32[]{:S(2)}) %collective-permute-start.4) | collective-permute-done | bytes 655392 | tf_op jit(solution)/shard_map/ppermute | solution.py:14
  190.0 2.8 select_maximum_fusion
  209.4 19.1 %copy.132 = f32[3,3,1280,320]{3,2,1,0:T(8,128)} copy(f32[3,3,1280,320]{2,3,1,0:T(8,128)} %bitcast.38) | data formatting | bytes 29491200 | tf_op jit(solution)/shard_map/reshape | solution.py:55
  245.7 19.0 %copy.133 = f32[3,3,1280,320]{3,2,1,0:T(8,128)} copy(f32[3,3,1280,320]{2,3,1,0:T(8,128)} %bitcast.58) | data formatting | bytes 29491200 | tf_op jit(solution)/shard_map/reshape | solution.py:55
  265.8 13.1 %all_gather.12 = bf16[2,128,1280]{1,0,2:T(2,128)(2,1)S(1)} all-gather(bf16[2,128,320]{1,0,2:T(2,128)(2,1)S(1)} %copy.104), channel_id=1, replica_groups=mesh['rows'=32,'chan'=4] {'chan'}, dimensions={2}, use_global_device_ids=true | all-gather | bytes 819200 | tf_op jit(solution)/shard_map/all_gather | solution.py:91
  282.8 3.2 copy.137
  286.0 3.4 pad.7.clone
  289.4 2.7 reshape.47
  292.6 9.1 fusion.58
  304.6 318.1 %reduce-scatter.3.cloned.1.call-done = f32[3,3,40,320]{3,2,1,0:T(8,128)} async-done(((f32[3,3,1280,320]{3,2,1,0:T(8,128)}), f32[3,3,40,320]{3,2,1,0:T(8,128)}) %reduce-scatter.3.cloned.1.call-update) | async-done | bytes 460816 | tf_op jit(solution)/shard_map/reduce_scatter | solution.py:117
  624.7 383.1 %reduce-scatter.5.cloned.1.call-done = f32[3,3,40,320]{3,2,1,0:T(8,128)} async-done(((f32[3,3,1280,320]{3,2,1,0:T(8,128)}), f32[3,3,40,320]{3,2,1,0:T(8,128)}) %reduce-scatter.5.cloned.1.call-update) | async-done | bytes 460816 | tf_op jit(solution)/shard_map/reduce_scatter | solution.py:111
  (104 shorter events, 71.3 us)
Async XLA Ops:
  7.2 45.7 %all-gather.3.cloned.1.call-start = ((), (), s32[]{:S(2)}) async-start(), calls=%async_computation.2 | async-start | bytes 1638400 | tf_op jit(solution)/shard_map/all_gather | solution.py:75
  8.2 10.9 %collective-permute-start.1 = (bf16[1,128,320]{1,2,0:T(8,128)(2,1)S(1)}, bf16[1,128,320]{1,2,0:T(8,128)(2,1)S(1)}, u32[]{:S(2)}, u32[]{:S(2)}) collective-permute-start(bf16[1,128,320]{1,2,0:T(8,128)(2,1)S(1)} %get-tuple-element.31), channel_id=1, source_target_pairs={{4,0},{8,4},{12,8},{16,12},{20,16},{24,20},{28,24},{32,28},{36,32}... | collective-permute-start | bytes 245768 | tf_op jit(solution)/shard_map/ppermute | solution.py:15
  14.9 9.3 collective-permute-start
  19.0 94.6 %all-reduce.6.cloned.1.call-start = ((), (), s32[]{:S(2)}) async-start(), calls=%async_computation.6 | async-start | bytes 5242880
  25.3 0.9 copy-start.9
  37.8 0.9 copy-start.6
  37.8 1.9 copy-start.8
  37.8 3.1 copy-start.5
  37.9 107.0 %all-gather.5.cloned.1.call-start = ((), (), s32[]{:S(2)}) async-start(), calls=%async_computation.3 | async-start | bytes 1638400 | tf_op jit(solution)/shard_map/all_gather | solution.py:90
  76.6 48.0 %copy-start.3 = (bf16[4,128,1280]{1,0,2:T(4,128)(2,1)S(1)}, bf16[4,128,1280]{1,0,2:T(4,128)(2,1)}, u32[]{:S(2)}) copy-start(bf16[4,128,1280]{1,0,2:T(4,128)(2,1)} %all-gather.3.cloned.1.call-done) | copy-start | bytes 3932164
  117.2 185.1 %all-reduce.8.cloned.1.call-start = ((), (), s32[]{:S(2)}) async-start(), calls=%async_computation.7 | async-start | bytes 5242880
  117.3 8.9 collective-permute-start.3
  122.1 9.5 collective-permute-start.2
  147.5 7.2 copy-start
  148.7 19.9 %collective-permute-start.5 = (bf16[2,1,128,1280]{3,2,1,0:T(8,128)(2,1)}, bf16[2,1,128,1280]{3,2,1,0:T(8,128)(2,1)}, u32[]{:S(2)}, u32[]{:S(2)}) collective-permute-start(bf16[2,1,128,1280]{3,2,1,0:T(8,128)(2,1)} %get-tuple-element.19), channel_id=1, source_target_pairs={{4,0},{8,4},{12,8},{16,12},{20,16},{24,20},{28,24},{32,28},{36,32}... | collective-permute-start | bytes 1966088 | tf_op jit(solution)/shard_map/ppermute | solution.py:15
  150.7 39.3 %collective-permute-start.4 = (bf16[2,1,128,1280]{3,2,1,0:T(8,128)(2,1)}, bf16[2,1,128,1280]{3,2,1,0:T(8,128)(2,1)}, u32[]{:S(2)}, u32[]{:S(2)}) collective-permute-start(bf16[2,1,128,1280]{3,2,1,0:T(8,128)(2,1)} %get-tuple-element.18), channel_id=1, source_target_pairs={{0,4},{4,8},{8,12},{12,16},{16,20},{20,24},{24,28},{28,32},{32,36}... | collective-permute-start | bytes 1966088 | tf_op jit(solution)/shard_map/ppermute | solution.py:14
  160.7 462.1 %reduce-scatter.3.cloned.1.call-start = ((), (), s32[]{:S(2)}) async-start(), calls=%async_computation.4 | async-start | bytes 18247680 | tf_op jit(solution)/shard_map/reduce_scatter | solution.py:117
  228.5 1.0 copy-start.1
  228.6 779.2 %reduce-scatter.5.cloned.1.call-start = ((), (), s32[]{:S(2)}) async-start(), calls=%async_computation.5 | async-start | bytes 18247680 | tf_op jit(solution)/shard_map/reduce_scatter | solution.py:111
  264.7 0.9 copy-start.7
  265.7 14.8 %copy-start.2 = (bf16[4,128,1280]{1,0,2:T(4,128)(2,1)S(1)}, bf16[4,128,1280]{1,0,2:T(4,128)(2,1)}, u32[]{:S(2)}) copy-start(bf16[4,128,1280]{1,0,2:T(4,128)(2,1)} %all-gather.5.cloned.1.call-done) | copy-start | bytes 3932164
  301.6 1.8 copy-start.4
Sparse Core Ops, SparseCore 0:
  19.1 24.3 all-gather.2
  46.1 67.4 all-reduce.5
  117.3 21.6 all-gather.4
  160.8 73.8 all-reduce.7
  237.0 385.7 reduce-scatter.2
  625.1 382.6 reduce-scatter.4
where the time goes:
time: 1030 us; the launch traced here: 1020 us
  waiting for transfers between devices  778 us (76%)
  local copies, waits for them, and re-layouts  89.4 us (9%)
  matrix products  65.8 us (6%)
  other arithmetic  22.5 us (2%)
  blocking collectives  22.5 us (2%)
  starting transfers between devices  22.3 us (2%)
  between operations  16.1 us (2%)
    reduce_scatter x1, waiting for transfers between devices, on_device(): lax.psum_scatter(tap_sums(rim_fields[1], cotangent), 'rows', scatter_dime...  383 us
    reduce_scatter x1, waiting for transfers between devices, on_device(): lax.psum_scatter(tap_sums(rim_fields[0], delta), 'rows', scatter_dimensio...  318 us
    reshape x2, local copies, waits for them, and re-layouts, tap_sums(): return stacked.reshape(3, 3, stacked.shape[1], out_width)  38.1 us
    unnamed x8, waiting for transfers between devices  37.1 us
    conv_general_dilated x4, matrix products, conv_rows(): lax.conv_general_dilated(padded[None], kernel, (1, 1), ((0, 0), (1, 1)),...  33.3 us
    dot_general x18, matrix products, tap_sums(): lax.dot_general(window, flat_grads, (((0,), (0,)), ((), ())), preferred_e...  32.5 us
    ppermute x3, waiting for transfers between devices, extended(): before = lax.ppermute(last, axis, up)  32 us
  transfers between devices with their start and end apart: 12, of which 7 were waited for; matrix products, arithmetic and copies ran while one was open for 16% of the time, Pallas kernels for 0%

commit v1 on v0

v1 whole, which is shorter than its diff:
```python
import jax
import jax.numpy as jnp
from jax import lax
from jax.sharding import Mesh
from jax.sharding import PartitionSpec as P

ROWS = ("ry", "rk")


def extended(shard, axis, peers, dim, width):
    length = shard.shape[dim]
    up = [(i, (i + 1) % peers) for i in range(peers - 1)]
    down = [(j, i) for i, j in up]
    last = lax.slice_in_dim(shard, length - width, length, axis=dim)
    leading = lax.slice_in_dim(shard, 0, width, axis=dim)
    before = lax.ppermute(last, axis, up)
    after = lax.ppermute(leading, axis, down)
    return jnp.concatenate([before, shard, after], axis=dim)


def silu_slope(values):
    logistic = jax.nn.sigmoid(values)
    return logistic * (1.0 + values * (1.0 - logistic))


def conv_rows(padded, kernel):
    result = lax.conv_general_dilated(
        padded[None],
        kernel,
        (1, 1),
        ((0, 0), (1, 1)),
        dimension_numbers=("NHWC", "HWIO", "NHWC"),
        preferred_element_type=jnp.float32,
    )
    return result[0]


def flipped(kernel):
    return jnp.transpose(kernel[::-1, ::-1], (0, 1, 3, 2))


def weight_grad(field_ext, grads, groups):
    rows, cols, out_width = grads.shape
    width = field_ext.shape[2] // groups
    pieces = field_ext.reshape(rows + 2, cols, groups, width).transpose(2, 0, 1, 3)
    fields = lax.all_to_all(pieces, "ry", 0, 0, tiled=True)
    fields = jnp.pad(fields, ((0, 0), (0, 0), (1, 1), (0, 0)))
    grads_all = lax.all_gather(grads, "ry", axis=0, tiled=False)
    flat_grads = grads_all.reshape(groups * rows * cols, out_width)
    taps = []
    for row_tap in range(3):
        for col_tap in range(3):
            window = fields[:, row_tap : row_tap + rows, col_tap : col_tap + cols]
            window = window.reshape(groups * rows * cols, width)
            taps.append(
                lax.dot_general(
                    window, flat_grads, (((0,), (0,)), ((), ())), preferred_element_type=jnp.float32
                )
            )
    partial = jnp.stack(taps).reshape(3, 3, width, out_width)
    return lax.psum_scatter(partial, "rk", scatter_dimension=2, tiled=True)


def make_body(groups, row_devices):
    def on_device(
        latent,
        stale_latent,
        stale_hidden,
        first_kernel,
        second_kernel,
        scale_table,
        timestep,
        cotangent,
    ):
        row_index = lax.axis_index(ROWS)
        height = latent.shape[0] * row_devices
        latent_f = latent.astype(jnp.float32)
        act = jax.nn.silu(latent_f).astype(jnp.bfloat16)
        edge_act = jax.nn.silu(stale_latent.astype(jnp.float32)).astype(jnp.bfloat16)
        act_all, edge_all = (
            lax.all_gather(act, "chan", axis=2, tiled=True),
            lax.all_gather(edge_act, "chan", axis=2, tiled=True),
        )

        def stale_pad(field, edges):
            above = jnp.where(row_index > 0, edges[0], jnp.zeros_like(edges[0]))
            below = jnp.where(row_index < row_devices - 1, edges[1], jnp.zeros_like(edges[1]))
            return jnp.concatenate([above[None], field, below[None]], axis=0)

        pre_act = conv_rows(stale_pad(act_all, edge_all), first_kernel)
        steps_iota = jnp.arange(scale_table.shape[0])[:, None]
        step_scale = jnp.sum(jnp.where(steps_iota == timestep[0], scale_table, 0.0), axis=0)
        scaled = pre_act * step_scale
        hidden = jax.nn.silu(scaled).astype(jnp.bfloat16)
        hidden_all, edge_hidden = (
            lax.all_gather(hidden, "chan", axis=2, tiled=True),
            lax.all_gather(stale_hidden, "chan", axis=2, tiled=True),
        )
        output = (latent_f + conv_rows(stale_pad(hidden_all, edge_hidden), second_kernel)).astype(
            jnp.bfloat16
        )
        grad_pad = extended(cotangent, ROWS, row_devices, 0, 1)
        grad_hidden = lax.psum_scatter(
            conv_rows(grad_pad, flipped(second_kernel)), "chan", scatter_dimension=2, tiled=True
        )
        delta = (grad_hidden * silu_slope(scaled) * step_scale).astype(jnp.bfloat16)
        delta_pad = extended(delta, ROWS, row_devices, 0, 1)
        grad_pre = lax.psum_scatter(
            conv_rows(delta_pad, flipped(first_kernel)), "chan", scatter_dimension=2, tiled=True
        )
        grad_latent = (
            latent_f * 0.0 + cotangent.astype(jnp.float32) + grad_pre * silu_slope(latent_f)
        ).astype(jnp.bfloat16)
        rim_fields = extended(jnp.stack((act_all, hidden_all)), ROWS, row_devices, 1, 1)
        grad_second = weight_grad(rim_fields[1], cotangent, groups) / height
        grad_first = weight_grad(rim_fields[0], delta, groups) / height
        return (output, grad_latent, grad_first, grad_second)

    return on_device


def solution(mesh):
    row_devices, chan_devices = mesh.devices.shape
    groups = 4
    sub = Mesh(mesh.devices.reshape(groups, row_devices // groups, chan_devices), ("ry", "rk", "chan"))
    rows_spec = P(ROWS, None, "chan")
    in_specs = (
        rows_spec,
        rows_spec,
        rows_spec,
        P(None, None, None, "chan"),
        P(None, None, None, "chan"),
        P(None, "chan"),
        P(),
        rows_spec,
    )
    out_specs = (
        rows_spec,
        rows_spec,
        P(None, None, ROWS, "chan"),
        P(None, None, ROWS, "chan"),
    )
    return jax.shard_map(
        make_body(groups, row_devices), mesh=sub, in_specs=in_specs, out_specs=out_specs, check_vma=False
    )
```

time: 1030 us -> 500 us (0.49)
  waiting for transfers between devices: 778 us -> 263 us
  local copies, waits for them, and re-layouts: 89.4 us -> 58 us
  starting transfers between devices: 22.3 us -> 34.7 us
  matrix products: 65.8 us -> 77.1 us
    reduce_scatter x2, waiting for transfers between devices: 701 us -> 139 us  [weight_grad(): return lax.psum_scatter(partial, 'rk', scatter_dimension=2, tiled=True)]
    reshape x2 -> x0, local copies, waits for them, and re-layouts: 38.1 us -> none  [tap_sums(): return stacked.reshape(3, 3, stacked.shape[1], out_width)]
    all_to_all x0 -> x2, waiting for transfers between devices: none -> 36.4 us  [weight_grad(): fields = lax.all_to_all(pieces, 'ry', 0, 0, tiled=True)]
    ppermute x3, waiting for transfers between devices: 32 us -> 8.11 us  [extended(): before = lax.ppermute(last, axis, up)]
    all_gather x1, waiting for transfers between devices: 0.01 us -> 21 us  [on_device(): lax.all_gather(hidden, 'chan', axis=2, tiled=True)]
    dot_general x18, matrix products: 32.5 us -> 43.8 us  [weight_grad(): lax.dot_general(window, flat_grads, (((0,), (0,)), ((), ())), preferred_e...]
    unnamed x8 -> x10, waiting for transfers between devices: 37.1 us -> 40.4 us
  transfers between devices with their start and end apart: 12 -> 16, of which waited for: 7 -> 9; matrix products, arithmetic and copies ran while one was open for 16% -> 30% of each run, Pallas kernels for 0% -> 0%
where the time goes in v1:
time: 500 us; the launch traced here: 493 us
  waiting for transfers between devices  263 us (53%)
  matrix products  77.1 us (15%)
  local copies, waits for them, and re-layouts  58 us (12%)
  starting transfers between devices  34.7 us (7%)
  blocking collectives  23 us (5%)
  other arithmetic  20.7 us (4%)
  between operations  16.2 us (3%)
    reduce_scatter x2, waiting for transfers between devices, weight_grad(): return lax.psum_scatter(partial, 'rk', scatter_dimension=2, tiled=True)  139 us
    dot_general x18, matrix products, weight_grad(): lax.dot_general(window, flat_grads, (((0,), (0,)), ((), ())), preferred_e...  43.8 us
    unnamed x10, waiting for transfers between devices  40.4 us
    all_to_all x2, waiting for transfers between devices, weight_grad(): fields = lax.all_to_all(pieces, 'ry', 0, 0, tiled=True)  36.4 us
    conv_general_dilated x4, matrix products, conv_rows(): lax.conv_general_dilated(padded[None], kernel, (1, 1), ((0, 0), (1, 1)),...  33.3 us
    all_gather x1, waiting for transfers between devices, on_device(): lax.all_gather(hidden, 'chan', axis=2, tiled=True)  21 us
    ppermute x3, starting transfers between devices, extended(): after = lax.ppermute(leading, axis, down)  18.5 us
    ppermute x3, waiting for transfers between devices, extended(): after = lax.ppermute(leading, axis, down)  17.9 us
  transfers between devices with their start and end apart: 16, of which 9 were waited for; matrix products, arithmetic and copies ran while one was open for 30% of the time, Pallas kernels for 0%

profile of v1, /device:TPU:8, one launch (start us, length us, event | category | flops | bytes accessed | tf_op | source)
XLA Modules:
  0.0 492.8 jit_solution(2391937284150672101)
XLA Ops:
  8.2 6.8 %collective-permute-start.1 = (bf16[1,128,320]{1,2,0:T(8,128)(2,1)S(1)}, bf16[1,128,320]{1,2,0:T(8,128)(2,1)S(1)}, u32[]{:S(2)}, u32[]{:S(2)}) collective-permute-start(bf16[1,128,320]{1,2,0:T(8,128)(2,1)S(1)} %get-tuple-element.27), channel_id=1, source_target_pairs={{4,0},{8,4},{12,8},{16,12},{20,16},{24,20},{28,24},{32,28},{36,32}... | collective-permute-start | bytes 245768 | tf_op jit(solution)/shard_map/ppermute | solution.py:17
  19.1 5.2 %collective-permute-done = bf16[1,128,320]{1,2,0:T(8,128)(2,1)S(1)} collective-permute-done((bf16[1,128,320]{1,2,0:T(8,128)(2,1)S(1)}, bf16[1,128,320]{1,2,0:T(8,128)(2,1)S(1)}, u32[]{:S(2)}, u32[]{:S(2)}) %collective-permute-start) | collective-permute-done | bytes 81952 | tf_op jit(solution)/shard_map/ppermute | solution.py:16
  25.4 7.6 %convolution_select_fusion.1 = f32[4,8,17,1280]{3,1,2,0:T(8,128)S(1)} fusion(bf16[3,3,1280,320]{2,3,1,0:T(8,128)(2,1)} %param.12, pred[8,17]{0,1:T(8,128)(4,1)S(1)} %copy-done.15, bf16[6,1,7,2,320]{4,2,3,0,1:T(8,128)(2,1)S(1)} %slice.142, bf16[6,1,8,17,320]{4,2,3,0,1:T(8,128)(2,1)S(1)} %copy.92), kind=kOutput, calls=%fused_computation.17 | convolution fusion | flops 4013250560 | bytes 10734216 | tf_op jit(solution)/shard_map/conv_general_dilated | solution.py:27
  40.4 9.3 %all_gather.25 = bf16[2,128,1280]{1,0,2:T(2,128)(2,1)S(1)} all-gather(bf16[2,128,320]{1,0,2:T(2,128)(2,1)S(1)} %copy.77), channel_id=1, replica_groups=mesh['ry'=4,'rk'=8,'chan'=4] {'chan'}, dimensions={2}, use_global_device_ids=true | all-gather | bytes 819200 | tf_op jit(solution)/shard_map/all_gather | solution.py:82
  51.9 3.4 maximum_bitcast_fusion
  55.4 3.2 copy.130
  58.5 3.4 pad.9.clone
  65.1 9.1 %fusion.33 = f32[4,8,17,320]{3,1,2,0:T(8,128)S(1)} fusion(bf16[3,3,1280,320]{2,3,1,0:T(8,128)(2,1)} %param.11, bf16[6,1,7,2,1280]{4,2,3,0,1:T(8,128)(2,1)S(1)} %slice.137, bf16[6,1,8,17,1280]{4,2,3,0,1:T(8,128)(2,1)S(1)} %copy.81, pred[8,17]{0,1:T(8,128)(4,1)S(1)} %copy-done.15), kind=kOutput, calls=%fused_computation.64 | convolution fusion | flops 4017981440 | bytes 10373256 | tf_op jit(solution)/shard_map/conv_general_dilated | solution.py:27
  74.8 39.7 %all-reduce.7.cloned.1.call-done = f32[4,128,1280]{1,0,2:T(4,128)} async-done(((f32[4,128,1280]{1,0,2:T(4,128)}), f32[4,128,1280]{1,0,2:T(4,128)}) %all-reduce.7.cloned.1.call-update) | async-done | bytes 2621456
  118.7 21.0 %all-gather.9.cloned.1.call-done = bf16[4,128,1280]{1,0,2:T(4,128)(2,1)} async-done(((bf16[4,128,320]{1,0,2:T(4,128)(2,1)}), bf16[4,128,1280]{1,0,2:T(4,128)(2,1)}) %all-gather.9.cloned.1.call-update) | async-done | bytes 1310736 | tf_op jit(solution)/shard_map/all_gather | solution.py:96
  144.5 4.8 collective-permute-start.5
  153.5 6.9 %collective-permute-start.3 = (bf16[1,128,320]{1,2,0:T(8,128)(2,1)S(1)}, bf16[1,128,320]{1,2,0:T(8,128)(2,1)S(1)}, u32[]{:S(2)}, u32[]{:S(2)}) collective-permute-start(bf16[1,128,320]{1,2,0:T(8,128)(2,1)S(1)} %get-tuple-element.25), channel_id=1, source_target_pairs={{4,0},{8,4},{12,8},{16,12},{20,16},{24,20},{28,24},{32,28},{36,32}... | collective-permute-start | bytes 245768 | tf_op jit(solution)/shard_map/ppermute | solution.py:17
  162.6 17.9 %collective-permute-done.3 = bf16[1,128,320]{1,2,0:T(8,128)(2,1)S(1)} collective-permute-done((bf16[1,128,320]{1,2,0:T(8,128)(2,1)S(1)}, bf16[1,128,320]{1,2,0:T(8,128)(2,1)S(1)}, u32[]{:S(2)}, u32[]{:S(2)}) %collective-permute-start.3) | collective-permute-done | bytes 81952 | tf_op jit(solution)/shard_map/ppermute | solution.py:17
  197.2 5.0 %all-to-all-start = ((bf16[4,6,128,320]{2,3,1,0:T(8,128)(2,1)}), bf16[4,6,128,320]{2,3,1,0:T(8,128)(2,1)}, u32[]{:S(2)}, u32[]{:S(2)}) async-start(bf16[4,6,128,320]{2,3,1,0:T(8,128)(2,1)} %bitcast.245), calls=%async_computation | async-start | bytes 3932160 | tf_op jit(solution)/shard_map/all_to_all | solution.py:46
  202.2 7.5 %convolution_select_fusion = f32[4,8,17,1280]{3,1,2,0:T(8,128)S(1)} fusion(bf16[3,3,1280,320]{2,3,1,0:T(8,128)(2,1)} %param.11, pred[8,17]{0,1:T(8,128)(4,1)S(1)} %copy-done.15, bf16[6,1,7,2,320]{4,2,3,0,1:T(8,128)(2,1)S(1)} %slice.146, bf16[6,1,8,17,320]{4,2,3,0,1:T(8,128)(2,1)S(1)} %copy-done.9), kind=kOutput, calls=%fused_computation.16 | convolution fusion | flops 4013250560 | bytes 10734216 | tf_op jit(solution)/shard_map/conv_general_dilated | solution.py:27
  214.2 13.4 %all-to-all-done = bf16[4,6,128,320]{2,3,1,0:T(8,128)(2,1)} async-done(((bf16[4,6,128,320]{2,3,1,0:T(8,128)(2,1)}), bf16[4,6,128,320]{2,3,1,0:T(8,128)(2,1)}, u32[]{:S(2)}, u32[]{:S(2)}) %all-to-all-start) | async-done | bytes 1966112 | tf_op jit(solution)/shard_map/all_to_all | solution.py:46
  227.6 3.4 fusion.59
  231.0 3.0 fusion.65
  234.0 3.0 fusion.57
  237.0 3.0 fusion.55
  243.0 3.0 fusion.53
  246.0 3.0 fusion.51
  252.0 3.0 fusion.49
  258.0 4.3 all-to-all-start.1
  262.8 23.0 %all-to-all-done.1 = bf16[4,6,128,320]{2,3,1,0:T(8,128)(2,1)S(1)} async-done(((bf16[4,6,128,320]{2,3,1,0:T(8,128)(2,1)}), bf16[4,6,128,320]{2,3,1,0:T(8,128)(2,1)S(1)}, u32[]{:S(2)}, u32[]{:S(2)}) %all-to-all-start.1) | async-done | bytes 1966112 | tf_op jit(solution)/shard_map/all_to_all | solution.py:46
  285.8 3.0 fusion.47
  303.3 13.8 %all_gather.24 = bf16[2,128,1280]{1,0,2:T(2,128)(2,1)S(1)} all-gather(bf16[2,128,320]{1,0,2:T(2,128)(2,1)S(1)} %copy.76), channel_id=1, replica_groups=mesh['ry'=4,'rk'=8,'chan'=4] {'chan'}, dimensions={2}, use_global_device_ids=true | all-gather | bytes 819200 | tf_op jit(solution)/shard_map/all_gather | solution.py:97
  320.9 3.2 copy.131
  324.2 3.3 pad.11.clone
  330.7 9.1 %fusion.30 = f32[4,8,17,320]{3,1,2,0:T(8,128)S(1)} fusion(bf16[3,3,1280,320]{2,3,1,0:T(8,128)(2,1)} %param.12, bf16[6,1,7,2,1280]{4,2,3,0,1:T(8,128)(2,1)S(1)} %slice.140, bf16[6,1,8,17,1280]{4,2,3,0,1:T(8,128)(2,1)S(1)} %copy.87, pred[8,17]{0,1:T(8,128)(4,1)S(1)} %copy-done.15), kind=kOutput, calls=%fused_computation.63 | convolution fusion | flops 4017981440 | bytes 10373256 | tf_op jit(solution)/shard_map/conv_general_dilated | solution.py:27
  342.8 42.4 %reduce-scatter.3.cloned.1.call-done = f32[3,3,40,320]{3,2,1,0:T(8,128)} async-done(((f32[3,3,320,320]{3,2,1,0:T(8,128)}), f32[3,3,40,320]{3,2,1,0:T(8,128)}) %reduce-scatter.3.cloned.1.call-update) | async-done | bytes 460816 | tf_op jit(solution)/shard_map/reduce_scatter | solution.py:61
  387.2 96.7 %reduce-scatter.5.cloned.1.call-done = f32[3,3,40,320]{3,2,1,0:T(8,128)} async-done(((f32[3,3,320,320]{3,2,1,0:T(8,128)}), f32[3,3,40,320]{3,2,1,0:T(8,128)}) %reduce-scatter.5.cloned.1.call-update) | async-done | bytes 460816 | tf_op jit(solution)/shard_map/reduce_scatter | solution.py:61
  (130 shorter events, 92.1 us)
Async XLA Ops:
  7.2 17.2 %copy-start.3 = (bf16[4,128,320]{1,2,0:T(8,128)(2,1)S(1)}, bf16[4,128,320]{1,2,0:T(8,128)(2,1)}, u32[]{:S(2)}) copy-start(bf16[4,128,320]{1,2,0:T(8,128)(2,1)} %param.15) | copy-start | bytes 983044
  7.2 44.7 %all-gather.7.cloned.1.call-start = ((), (), s32[]{:S(2)}) async-start(), calls=%async_computation.4 | async-start | bytes 1638400 | tf_op jit(solution)/shard_map/all_gather | solution.py:81
  8.2 10.9 %collective-permute-start.1 = (bf16[1,128,320]{1,2,0:T(8,128)(2,1)S(1)}, bf16[1,128,320]{1,2,0:T(8,128)(2,1)S(1)}, u32[]{:S(2)}, u32[]{:S(2)}) collective-permute-start(bf16[1,128,320]{1,2,0:T(8,128)(2,1)S(1)} %get-tuple-element.27), channel_id=1, source_target_pairs={{4,0},{8,4},{12,8},{16,12},{20,16},{24,20},{28,24},{32,28},{36,32}... | collective-permute-start | bytes 245768 | tf_op jit(solution)/shard_map/ppermute | solution.py:17
  15.0 9.3 %collective-permute-start = (bf16[1,128,320]{1,2,0:T(8,128)(2,1)S(1)}, bf16[1,128,320]{1,2,0:T(8,128)(2,1)S(1)}, u32[]{:S(2)}, u32[]{:S(2)}) collective-permute-start(bf16[1,128,320]{1,2,0:T(8,128)(2,1)S(1)} %get-tuple-element.26), channel_id=1, source_target_pairs={{0,4},{4,8},{8,12},{12,16},{16,20},{20,24},{24,28},{28,32},{32,36}... | collective-permute-start | bytes 245768 | tf_op jit(solution)/shard_map/ppermute | solution.py:16
  19.1 95.5 %all-reduce.7.cloned.1.call-start = ((), (), s32[]{:S(2)}) async-start(), calls=%async_computation.10 | async-start | bytes 5242880
  24.7 0.7 copy-start.15
  37.0 0.9 copy-start.10
  37.0 1.9 copy-start.14
  37.0 3.1 copy-start.7
  37.1 102.6 %all-gather.9.cloned.1.call-start = ((), (), s32[]{:S(2)}) async-start(), calls=%async_computation.5 | async-start | bytes 1638400 | tf_op jit(solution)/shard_map/all_gather | solution.py:96
  74.8 43.7 %copy-start.2 = (bf16[4,128,1280]{1,0,2:T(4,128)(2,1)S(1)}, bf16[4,128,1280]{1,0,2:T(4,128)(2,1)}, u32[]{:S(2)}) copy-start(bf16[4,128,1280]{1,0,2:T(4,128)(2,1)} %all-gather.7.cloned.1.call-done) | copy-start | bytes 3932164
  117.9 96.3 %all-gather.11.cloned.1.call-start = ((), (), s32[]{:S(2)}) async-start(), calls=%async_computation.8 | async-start | bytes 1638400 | tf_op jit(solution)/shard_map/all_gather | solution.py:48
  118.4 144.4 %all-gather.13.cloned.1.call-start = ((), (), s32[]{:S(2)}) async-start(), calls=%async_computation.9 | async-start | bytes 1638400 | tf_op jit(solution)/shard_map/all_gather | solution.py:48
  142.3 11.2 %copy-start.5 = (bf16[4,128,320]{1,2,0:T(8,128)(2,1)S(1)}, bf16[4,128,320]{1,2,0:T(8,128)(2,1)}, u32[]{:S(2)}) copy-start(bf16[4,128,320]{1,2,0:T(8,128)(2,1)} %get-tuple-element.16) | copy-start | bytes 983044
  144.5 44.5 %collective-permute-start.5 = (bf16[2,1,128,1280]{3,2,1,0:T(8,128)(2,1)}, bf16[2,1,128,1280]{3,2,1,0:T(8,128)(2,1)}, u32[]{:S(2)}, u32[]{:S(2)}) collective-permute-start(bf16[2,1,128,1280]{3,2,1,0:T(8,128)(2,1)} %copy.105), channel_id=1, source_target_pairs={{4,0},{8,4},{12,8},{16,12},{20,16},{24,20},{28,24},{32,28},{36,32}... | collective-permute-start | bytes 1966088 | tf_op jit(solution)/shard_map/ppermute | solution.py:17
  151.6 38.8 %collective-permute-start.4 = (bf16[2,1,128,1280]{3,2,1,0:T(8,128)(2,1)}, bf16[2,1,128,1280]{3,2,1,0:T(8,128)(2,1)}, u32[]{:S(2)}, u32[]{:S(2)}) collective-permute-start(bf16[2,1,128,1280]{3,2,1,0:T(8,128)(2,1)} %copy.104), channel_id=1, source_target_pairs={{0,4},{4,8},{8,12},{12,16},{16,20},{20,24},{24,28},{28,32},{32,36}... | collective-permute-start | bytes 1966088 | tf_op jit(solution)/shard_map/ppermute | solution.py:16
  153.5 27.0 %collective-permute-start.3 = (bf16[1,128,320]{1,2,0:T(8,128)(2,1)S(1)}, bf16[1,128,320]{1,2,0:T(8,128)(2,1)S(1)}, u32[]{:S(2)}, u32[]{:S(2)}) collective-permute-start(bf16[1,128,320]{1,2,0:T(8,128)(2,1)S(1)} %get-tuple-element.25), channel_id=1, source_target_pairs={{4,0},{8,4},{12,8},{16,12},{20,16},{24,20},{28,24},{32,28},{36,32}... | collective-permute-start | bytes 245768 | tf_op jit(solution)/shard_map/ppermute | solution.py:17
  160.4 23.0 %collective-permute-start.2 = (bf16[1,128,320]{1,2,0:T(8,128)(2,1)S(1)}, bf16[1,128,320]{1,2,0:T(8,128)(2,1)S(1)}, u32[]{:S(2)}, u32[]{:S(2)}) collective-permute-start(bf16[1,128,320]{1,2,0:T(8,128)(2,1)S(1)} %get-tuple-element.24), channel_id=1, source_target_pairs={{0,4},{4,8},{8,12},{12,16},{16,20},{20,24},{24,28},{28,32},{32,36}... | collective-permute-start | bytes 245768 | tf_op jit(solution)/shard_map/ppermute | solution.py:16
  188.2 0.8 copy-start.8
  197.2 5.0 %copy-start.9 = (bf16[6,1,8,17,320]{4,2,3,0,1:T(8,128)(2,1)S(1)}, bf16[6,1,8,17,320]{4,2,3,0,1:T(8,128)(2,1)}, u32[]{:S(2)}) copy-start(bf16[6,1,8,17,320]{4,2,3,0,1:T(8,128)(2,1)} %copy-done.8) | copy-start | bytes 1566724
  197.2 30.4 %all-to-all-start = ((bf16[4,6,128,320]{2,3,1,0:T(8,128)(2,1)}), bf16[4,6,128,320]{2,3,1,0:T(8,128)(2,1)}, u32[]{:S(2)}, u32[]{:S(2)}) async-start(bf16[4,6,128,320]{2,3,1,0:T(8,128)(2,1)} %bitcast.245), calls=%async_computation | async-start | bytes 3932160 | tf_op jit(solution)/shard_map/all_to_all | solution.py:46
  202.2 138.3 %all-reduce.9.cloned.1.call-start = ((), (), s32[]{:S(2)}) async-start(), calls=%async_computation.11 | async-start | bytes 5242880
  213.9 171.4 %reduce-scatter.3.cloned.1.call-start = ((), (), s32[]{:S(2)}) async-start(), calls=%async_computation.6 | async-start | bytes 4976640 | tf_op jit(solution)/shard_map/reduce_scatter | solution.py:61
  214.2 16.8 %copy-start.13 = (bf16[16,128,320]{1,2,0:T(8,128)(2,1)S(1)}, bf16[16,128,320]{1,2,0:T(8,128)(2,1)}, u32[]{:S(2)}) copy-start(bf16[16,128,320]{1,2,0:T(8,128)(2,1)} %all-gather.11.cloned.1.call-done) | copy-start | bytes 3932164
  255.0 1.5 copy-start
  258.0 27.8 %all-to-all-start.1 = ((bf16[4,6,128,320]{2,3,1,0:T(8,128)(2,1)}), bf16[4,6,128,320]{2,3,1,0:T(8,128)(2,1)S(1)}, u32[]{:S(2)}, u32[]{:S(2)}) async-start(bf16[4,6,128,320]{2,3,1,0:T(8,128)(2,1)} %bitcast.244), calls=%async_computation.2 | async-start | bytes 3932160 | tf_op jit(solution)/shard_map/all_to_all | solution.py:46
  262.3 221.6 %reduce-scatter.5.cloned.1.call-start = ((), (), s32[]{:S(2)}) async-start(), calls=%async_computation.7 | async-start | bytes 4976640 | tf_op jit(solution)/shard_map/reduce_scatter | solution.py:61
  262.8 26.0 %copy-start.12 = (bf16[16,128,320]{1,2,0:T(8,128)(2,1)S(1)}, bf16[16,128,320]{1,2,0:T(8,128)(2,1)}, u32[]{:S(2)}) copy-start(bf16[16,128,320]{1,2,0:T(8,128)(2,1)} %all-gather.13.cloned.1.call-done) | copy-start | bytes 3932164
  302.2 0.9 copy-start.11
  303.2 15.5 %copy-start.1 = (bf16[4,128,1280]{1,0,2:T(4,128)(2,1)S(1)}, bf16[4,128,1280]{1,0,2:T(4,128)(2,1)}, u32[]{:S(2)}) copy-start(bf16[4,128,1280]{1,0,2:T(4,128)(2,1)} %all-gather.9.cloned.1.call-done) | copy-start | bytes 3932164
  340.0 1.6 copy-start.4
  340.0 1.6 copy-start.6
Sparse Core Ops, SparseCore 0:
  19.2 24.3 all-gather.6
  46.1 68.4 all-reduce.6
  118.0 21.6 all-gather.8
  141.7 23.4 all-gather.10
  166.8 42.7 all-gather.12
  214.0 69.5 all-reduce.8
  286.0 99.2 reduce-scatter.2
  387.7 96.1 reduce-scatter.4

commit v2 on v1

--- a/solution.py
+++ b/solution.py
@@ -39,6 +39,11 @@
     return jnp.transpose(kernel[::-1, ::-1], (0, 1, 3, 2))
 
 
+def reduce_chunks(chunks, axis):
+    received = lax.all_to_all(chunks, axis, 0, 0, tiled=True)
+    return jnp.sum(received, axis=0)
+
+
 def weight_grad(field_ext, grads, groups):
     rows, cols, out_width = grads.shape
     width = field_ext.shape[2] // groups
@@ -57,8 +62,9 @@
                     window, flat_grads, (((0,), (0,)), ((), ())), preferred_element_type=jnp.float32
                 )
             )
-    partial = jnp.stack(taps).reshape(3, 3, width, out_width)
-    return lax.psum_scatter(partial, "rk", scatter_dimension=2, tiled=True)
+    parts = lax.axis_size("rk")
+    partial = jnp.stack([t.reshape(parts, width // parts, out_width) for t in taps], axis=1)
+    return reduce_chunks(partial, "rk").reshape(3, 3, width // parts, out_width)
 
 
 def make_body(groups, row_devices):
@@ -77,37 +83,34 @@
         latent_f = latent.astype(jnp.float32)
         act = jax.nn.silu(latent_f).astype(jnp.bfloat16)
         edge_act = jax.nn.silu(stale_latent.astype(jnp.float32)).astype(jnp.bfloat16)
-        act_all, edge_all = (
-            lax.all_gather(act, "chan", axis=2, tiled=True),
-            lax.all_gather(edge_act, "chan", axis=2, tiled=True),
-        )
+        def gathered(field, edges):
+            joined = jnp.concatenate([edges[0:1], field, edges[1:2]], axis=0)
+            joined = lax.all_gather(joined, "chan", axis=2, tiled=True)
+            rows = field.shape[0]
+            above = jnp.where(row_index > 0, joined[0:1], jnp.zeros_like(joined[0:1]))
+            below = jnp.where(row_index < row_devices - 1, joined[rows + 1 :], jnp.zeros_like(joined[0:1]))
+            middle = joined[1 : rows + 1]
+            return middle, jnp.concatenate([above, middle, below], axis=0)
 
-        def stale_pad(field, edges):
-            above = jnp.where(row_index > 0, edges[0], jnp.zeros_like(edges[0]))
-            below = jnp.where(row_index < row_devices - 1, edges[1], jnp.zeros_like(edges[1]))
-            return jnp.concatenate([above[None], field, below[None]], axis=0)
+        def chan_reduce(values):
+            rows, cols, width = values.shape
+            parts = lax.axis_size("chan")
+            chunks = values.reshape(rows, cols, parts, width // parts).transpose(2, 0, 1, 3)
+            return reduce_chunks(chunks, "chan")
 
-        pre_act = conv_rows(stale_pad(act_all, edge_all), first_kernel)
+        act_all, act_pad = gathered(act, edge_act)
+        pre_act = conv_rows(act_pad, first_kernel)
         steps_iota = jnp.arange(scale_table.shape[0])[:, None]
         step_scale = jnp.sum(jnp.where(steps_iota == timestep[0], scale_table, 0.0), axis=0)
         scaled = pre_act * step_scale
         hidden = jax.nn.silu(scaled).astype(jnp.bfloat16)
-        hidden_all, edge_hidden = (
-            lax.all_gather(hidden, "chan", axis=2, tiled=True),
-            lax.all_gather(stale_hidden, "chan", axis=2, tiled=True),
-        )
-        output = (latent_f + conv_rows(stale_pad(hidden_all, edge_hidden), second_kernel)).astype(
-            jnp.bfloat16
-        )
+        hidden_all, hidden_pad = gathered(hidden, stale_hidden)
+        output = (latent_f + conv_rows(hidden_pad, second_kernel)).astype(jnp.bfloat16)
         grad_pad = extended(cotangent, ROWS, row_devices, 0, 1)
-        grad_hidden = lax.psum_scatter(
-            conv_rows(grad_pad, flipped(second_kernel)), "chan", scatter_dimension=2, tiled=True
-        )
+        grad_hidden = chan_reduce(conv_rows(grad_pad, flipped(second_kernel)))
         delta = (grad_hidden * silu_slope(scaled) * step_scale).astype(jnp.bfloat16)
         delta_pad = extended(delta, ROWS, row_devices, 0, 1)
-        grad_pre = lax.psum_scatter(
-            conv_rows(delta_pad, flipped(first_kernel)), "chan", scatter_dimension=2, tiled=True
-        )
+        grad_pre = chan_reduce(conv_rows(delta_pad, flipped(first_kernel)))
         grad_latent = (
             latent_f * 0.0 + cotangent.astype(jnp.float32) + grad_pre * silu_slope(latent_f)
         ).astype(jnp.bfloat16)

time: 500 us -> 470 us (0.940)
  waiting for transfers between devices: 263 us -> 116 us
  local copies, waits for them, and re-layouts: 58 us -> 190 us
  blocking collectives: 23 us -> 0 us
  starting transfers between devices: 34.7 us -> 51.7 us
  matrix products: 77.1 us -> 61.8 us
  other arithmetic: 20.7 us -> 26 us
    reduce_scatter x2 -> x0, waiting for transfers between devices: 139 us -> none  [weight_grad(): return lax.psum_scatter(partial, 'rk', scatter_dimension=2, tiled=True)]
    reshape x0 -> x20, local copies, waits for them, and re-layouts: none -> 64.5 us  [the longest x18 61.3 us: weight_grad(): window = window.reshape(groups * rows * cols, width)]
    all_to_all x0 -> x4, waiting for transfers between devices: none -> 53 us  [reduce_chunks(): received = lax.all_to_all(chunks, axis, 0, 0, tiled=True)]
    slice x0 -> x22, local copies, waits for them, and re-layouts: none -> 45.1 us  [the longest x20 45 us: weight_grad(): window = fields[:, row_tap:row_tap + rows, col_tap:col_tap + cols]]
    unnamed x10 -> x4, waiting for transfers between devices: 40.4 us -> 0.73 us
    all_to_all x2, waiting for transfers between devices: 36.4 us -> 12.1 us  [weight_grad(): fields = lax.all_to_all(pieces, 'ry', 0, 0, tiled=True)]
    all_gather x2 -> x0, blocking collectives: 23 us -> none  [the longest x1 13.8 us: on_device(): lax.all_gather(stale_hidden, 'chan', axis=2, tiled=True)]
    all_to_all x0 -> x4, starting transfers between devices: none -> 19.7 us  [reduce_chunks(): received = lax.all_to_all(chunks, axis, 0, 0, tiled=True)]
  transfers between devices with their start and end apart: 16 -> 16, of which waited for: 9 -> 10; matrix products, arithmetic and copies ran while one was open for 30% -> 52% of each run, Pallas kernels for 0% -> 0%
where the time goes in v2:
time: 470 us; the launch traced here: 461 us
  local copies, waits for them, and re-layouts  190 us (40%)
  waiting for transfers between devices  116 us (25%)
  matrix products  61.8 us (13%)
  starting transfers between devices  51.7 us (11%)
  other arithmetic  26 us (6%)
  between operations  15.5 us (3%)
    reshape x18, local copies, waits for them, and re-layouts, weight_grad(): window = window.reshape(groups * rows * cols, width)  61.3 us
    all_to_all x4, waiting for transfers between devices, reduce_chunks(): received = lax.all_to_all(chunks, axis, 0, 0, tiled=True)  53 us
    slice x20, local copies, waits for them, and re-layouts, weight_grad(): window = fields[:, row_tap:row_tap + rows, col_tap:col_tap + cols]  45 us
    conv_general_dilated x4, matrix products, conv_rows(): lax.conv_general_dilated(padded[None], kernel, (1, 1), ((0, 0), (1, 1)),...  35 us
    dot_general x18, matrix products, weight_grad(): lax.dot_general(window, flat_grads, (((0,), (0,)), ((), ())), preferred_e...  26.8 us
    ppermute x3, waiting for transfers between devices, extended(): before = lax.ppermute(last, axis, up)  23.3 us
    all_gather x2, waiting for transfers between devices, gathered(): joined = lax.all_gather(joined, 'chan', axis=2, tiled=True)  22 us
    all_to_all x4, starting transfers between devices, reduce_chunks(): received = lax.all_to_all(chunks, axis, 0, 0, tiled=True)  19.7 us
  transfers between devices with their start and end apart: 16, of which 10 were waited for; matrix products, arithmetic and copies ran while one was open for 52% of the time, Pallas kernels for 0%

profile of v2, /device:TPU:8, one launch (start us, length us, event | category | flops | bytes accessed | tf_op | source)
XLA Modules:
  0.0 460.8 jit_solution(15759301504451622832)
XLA Ops:
  8.2 6.8 %collective-permute-start.1 = (bf16[1,128,320]{1,2,0:T(8,128)(2,1)S(1)}, bf16[1,128,320]{1,2,0:T(8,128)(2,1)S(1)}, u32[]{:S(2)}, u32[]{:S(2)}) collective-permute-start(bf16[1,128,320]{1,2,0:T(8,128)(2,1)S(1)} %get-tuple-element.53), channel_id=1, source_target_pairs={{4,0},{8,4},{12,8},{16,12},{20,16},{24,20},{28,24},{32,28},{36,32}... | collective-permute-start | bytes 245768 | tf_op jit(solution)/shard_map/ppermute | solution.py:17
  20.0 4.3 collective-permute-done
  25.5 7.6 %convolution_select_fusion.1 = f32[4,8,17,1280]{3,1,2,0:T(8,128)S(1)} fusion(bf16[3,3,1280,320]{2,3,1,0:T(8,128)(2,1)} %param.12, pred[8,17]{0,1:T(8,128)(4,1)S(1)} %copy-done.40, bf16[6,1,7,2,320]{4,2,3,0,1:T(8,128)(2,1)S(1)} %slice.171, bf16[6,1,8,17,320]{4,2,3,0,1:T(8,128)(2,1)S(1)} %copy.168), kind=kOutput, calls=%fused_computation.17 | convolution fusion | flops 4013250560 | bytes 10734216 | tf_op jit(solution)/shard_map/conv_general_dilated | solution.py:27
  40.6 4.0 all-to-all-start
  47.0 30.4 %all-to-all-done = f32[4,4,128,320]{2,3,1,0:T(8,128)S(1)} async-done(((f32[4,4,128,320]{2,3,1,0:T(8,128)}), f32[4,4,128,320]{2,3,1,0:T(8,128)S(1)}, u32[]{:S(2)}, u32[]{:S(2)}) %all-to-all-start) | async-done | bytes 2621472 | tf_op jit(solution)/shard_map/all_to_all | solution.py:43
  91.5 10.8 %add_multiply_fusion = (f32[4,8,17,320]{3,1,2,0:T(8,128)}, f32[4,8,17,320]{3,1,2,0:T(8,128)S(1)}) fusion(f32[320]{0:T(512)S(1)} %select_reduce_fusion, bf16[3,3,1280,320]{2,3,1,0:T(8,128)(2,1)} %param.11, bf16[6,1,7,2,1280]{4,2,3,0,1:T(8,128)(2,1)S(1)} %slice.164, bf16[6,1,8,17,1280]{4,2,3,0,1:T(8,128)(2,1)S(1)} %copy.158, pred[8,17]{0,1:T(8,128)(4,1)S(1)} %copy-done.40), kind=kOutput, calls=%fused_computation.81 | convolution fusion | flops 4019374080 | bytes 11070856 | tf_op jit(solution)/shard_map/conv_general_dilated | solution.py:27
  106.4 22.0 %all-gather.8.cloned.1.call-done = bf16[6,128,1280]{1,2,0:T(8,128)(2,1)} async-done(((bf16[6,128,320]{1,2,0:T(8,128)(2,1)}), bf16[6,128,1280]{1,2,0:T(8,128)(2,1)}) %all-gather.8.cloned.1.call-update) | async-done | bytes 1966096 | tf_op jit(solution)/shard_map/all_gather | solution.py:88
  134.5 4.8 %collective-permute-start.5 = (bf16[2,1,128,1280]{3,2,1,0:T(8,128)(2,1)}, bf16[2,1,128,1280]{3,2,1,0:T(8,128)(2,1)}, u32[]{:S(2)}, u32[]{:S(2)}) collective-permute-start(bf16[2,1,128,1280]{3,2,1,0:T(8,128)(2,1)} %copy.181), channel_id=1, source_target_pairs={{4,0},{8,4},{12,8},{16,12},{20,16},{24,20},{28,24},{32,28},{36,32}... | collective-permute-start | bytes 1966088 | tf_op jit(solution)/shard_map/ppermute | solution.py:17
  150.5 4.3 collective-permute-done.5
  156.2 13.8 %collective-permute-done.4 = bf16[2,1,128,1280]{3,2,1,0:T(8,128)(2,1)} collective-permute-done((bf16[2,1,128,1280]{3,2,1,0:T(8,128)(2,1)}, bf16[2,1,128,1280]{3,2,1,0:T(8,128)(2,1)}, u32[]{:S(2)}, u32[]{:S(2)}) %collective-permute-start.4) | collective-permute-done | bytes 655392 | tf_op jit(solution)/shard_map/ppermute | solution.py:16
  176.7 5.0 %all-to-all-start.2 = ((bf16[4,6,128,320]{2,3,1,0:T(8,128)(2,1)}), bf16[4,6,128,320]{2,3,1,0:T(8,128)(2,1)S(1)}, u32[]{:S(2)}, u32[]{:S(2)}) async-start(bf16[4,6,128,320]{2,3,1,0:T(8,128)(2,1)} %copy.184), calls=%async_computation.2 | async-start | bytes 3932160 | tf_op jit(solution)/shard_map/all_to_all | solution.py:51
  183.8 3.7 collective-permute-start.2
  188.0 5.2 %collective-permute-done.2 = bf16[1,128,320]{1,2,0:T(8,128)(2,1)S(1)} collective-permute-done((bf16[1,128,320]{1,2,0:T(8,128)(2,1)S(1)}, bf16[1,128,320]{1,2,0:T(8,128)(2,1)S(1)}, u32[]{:S(2)}, u32[]{:S(2)}) %collective-permute-start.2) | collective-permute-done | bytes 81952 | tf_op jit(solution)/shard_map/ppermute | solution.py:16
  194.2 7.6 %convolution_select_fusion = f32[4,8,17,1280]{3,1,2,0:T(8,128)S(1)} fusion(bf16[3,3,1280,320]{2,3,1,0:T(8,128)(2,1)} %param.11, pred[8,17]{0,1:T(8,128)(4,1)S(1)} %copy-done.40, bf16[6,1,7,2,320]{4,2,3,0,1:T(8,128)(2,1)S(1)} %slice.175, bf16[6,1,8,17,320]{4,2,3,0,1:T(8,128)(2,1)S(1)} %copy.175), kind=kOutput, calls=%fused_computation.16 | convolution fusion | flops 4013250560 | bytes 10734216 | tf_op jit(solution)/shard_map/conv_general_dilated | solution.py:27
  204.5 4.2 copy.177
  214.2 4.7 %all-to-all-start.1 = ((f32[4,4,128,320]{2,3,1,0:T(8,128)}), f32[4,4,128,320]{2,3,1,0:T(8,128)}, u32[]{:S(2)}, u32[]{:S(2)}) async-start(f32[4,4,128,320]{2,3,1,0:T(8,128)} %copy.178), calls=%async_computation.1 | async-start | bytes 5242880 | tf_op jit(solution)/shard_map/all_to_all | solution.py:43
  229.7 4.6 pad_slice_fusion.6
  242.2 3.6 reshape.192
  253.7 4.0 reshape.196
  259.9 3.6 reshape.198
  291.2 5.0 %all-to-all-start.4 = ((bf16[4,6,128,320]{2,3,1,0:T(8,128)(2,1)}), bf16[4,6,128,320]{2,3,1,0:T(8,128)(2,1)S(1)}, u32[]{:S(2)}, u32[]{:S(2)}) async-start(bf16[4,6,128,320]{2,3,1,0:T(8,128)(2,1)} %copy.198), calls=%async_computation.4 | async-start | bytes 3932160 | tf_op jit(solution)/shard_map/all_to_all | solution.py:51
  305.9 4.6 copy.197
  310.4 10.1 %all-to-all-done.4 = bf16[4,6,128,320]{2,3,1,0:T(8,128)(2,1)S(1)} async-done(((bf16[4,6,128,320]{2,3,1,0:T(8,128)(2,1)}), bf16[4,6,128,320]{2,3,1,0:T(8,128)(2,1)S(1)}, u32[]{:S(2)}, u32[]{:S(2)}) %all-to-all-start.4) | async-done | bytes 1966112 | tf_op jit(solution)/shard_map/all_to_all | solution.py:51
  320.6 5.0 %all-to-all-start.3 = ((f32[8,9,40,320]{3,2,1,0:T(8,128)}), f32[8,9,40,320]{3,2,1,0:T(8,128)}, u32[]{:S(2)}, u32[]{:S(2)}) async-start(f32[8,9,40,320]{3,2,1,0:T(8,128)} %copy.197), calls=%async_computation.3 | async-start | bytes 8847360 | tf_op jit(solution)/shard_map/all_to_all | solution.py:43
  325.6 4.7 %pad_slice_fusion = (bf16[4,4,128,320]{2,3,1,0:T(8,128)(2,1)S(1)}, bf16[4,4,128,320]{2,3,1,0:T(8,128)(2,1)}, bf16[4,4,128,320]{2,3,1,0:T(8,128)(2,1)}, bf16[4,4,...) fusion(bf16[4,6,128,320]{2,3,1,0:T(8,128)(2,1)S(1)} %all-to-all, ...), kind=kLoop, calls=%fused_computation | loop fusion | bytes 17694720 | tf_op jit(solution)/shard_map/slice | solution.py:58
  338.1 3.6 reshape.211
  343.7 3.6 reshape.213
  355.0 3.6 reshape.217
  360.7 3.8 reshape.219
  393.3 6.0 %all-to-all-start.5 = ((f32[8,9,40,320]{3,2,1,0:T(8,128)}), f32[8,9,40,320]{3,2,1,0:T(8,128)}, u32[]{:S(2)}, u32[]{:S(2)}) async-start(f32[8,9,40,320]{3,2,1,0:T(8,128)} %copy.209), calls=%async_computation.5 | async-start | bytes 8847360 | tf_op jit(solution)/shard_map/all_to_all | solution.py:43
  412.6 9.1 %fusion.18 = f32[4,8,17,320]{3,1,2,0:T(8,128)S(1)} fusion(bf16[3,3,1280,320]{2,3,1,0:T(8,128)(2,1)} %param.12, bf16[6,1,7,2,1280]{4,2,3,0,1:T(8,128)(2,1)S(1)} %slice.169, bf16[6,1,8,17,1280]{4,2,3,0,1:T(8,128)(2,1)S(1)} %copy.163, pred[8,17]{0,1:T(8,128)(4,1)S(1)} %copy-done.40), kind=kOutput, calls=%fused_computation.41 | convolution fusion | flops 4017981440 | bytes 10373256 | tf_op jit(solution)/shard_map/conv_general_dilated | solution.py:27
  427.8 22.6 %all-to-all-done.5 = f32[8,9,40,320]{3,2,1,0:T(8,128)} async-done(((f32[8,9,40,320]{3,2,1,0:T(8,128)}), f32[8,9,40,320]{3,2,1,0:T(8,128)}, u32[]{:S(2)}, u32[]{:S(2)}) %all-to-all-start.5) | async-done | bytes 3686432 | tf_op jit(solution)/shard_map/all_to_all | solution.py:43
  (225 shorter events, 208.8 us)
Async XLA Ops:
  7.2 71.3 %all-gather.6.cloned.1.call-start = ((), (), s32[]{:S(2)}) async-start(), calls=%async_computation.6 | async-start | bytes 2457600 | tf_op jit(solution)/shard_map/all_gather | solution.py:88
  8.2 11.8 %collective-permute-start.1 = (bf16[1,128,320]{1,2,0:T(8,128)(2,1)S(1)}, bf16[1,128,320]{1,2,0:T(8,128)(2,1)S(1)}, u32[]{:S(2)}, u32[]{:S(2)}) collective-permute-start(bf16[1,128,320]{1,2,0:T(8,128)(2,1)S(1)} %get-tuple-element.53), channel_id=1, source_target_pairs={{4,0},{8,4},{12,8},{16,12},{20,16},{24,20},{28,24},{32,28},{36,32}... | collective-permute-start | bytes 245768 | tf_op jit(solution)/shard_map/ppermute | solution.py:17
  14.9 9.3 %collective-permute-start = (bf16[1,128,320]{1,2,0:T(8,128)(2,1)S(1)}, bf16[1,128,320]{1,2,0:T(8,128)(2,1)S(1)}, u32[]{:S(2)}, u32[]{:S(2)}) collective-permute-start(bf16[1,128,320]{1,2,0:T(8,128)(2,1)S(1)} %get-tuple-element.52), channel_id=1, source_target_pairs={{0,4},{4,8},{8,12},{12,16},{16,20},{20,24},{24,28},{28,32},{32,36}... | collective-permute-start | bytes 245768 | tf_op jit(solution)/shard_map/ppermute | solution.py:16
  17.9 6.4 %copy-start.17 = (bf16[4,128,320]{1,2,0:T(8,128)(2,1)S(1)}, bf16[4,128,320]{1,2,0:T(8,128)(2,1)}, u32[]{:S(2)}) copy-start(bf16[4,128,320]{1,2,0:T(8,128)(2,1)} %param.15) | copy-start | bytes 983044
  40.6 36.8 %all-to-all-start = ((f32[4,4,128,320]{2,3,1,0:T(8,128)}), f32[4,4,128,320]{2,3,1,0:T(8,128)S(1)}, u32[]{:S(2)}, u32[]{:S(2)}) async-start(f32[4,4,128,320]{2,3,1,0:T(8,128)} %copy.171), calls=%async_computation | async-start | bytes 5242880 | tf_op jit(solution)/shard_map/all_to_all | solution.py:43
  44.6 83.7 %all-gather.8.cloned.1.call-start = ((), (), s32[]{:S(2)}) async-start(), calls=%async_computation.7 | async-start | bytes 2457600 | tf_op jit(solution)/shard_map/all_gather | solution.py:88
  105.6 113.3 %all-gather.12.cloned.1.call-start = ((), (), s32[]{:S(2)}) async-start(), calls=%async_computation.9 | async-start | bytes 1638400 | tf_op jit(solution)/shard_map/all_gather | solution.py:53
  106.3 24.8 %copy-start = (bf16[1,4,128,1280]{2,3,1,0:T(8,128)(2,1)S(1)}, bf16[1,4,128,1280]{2,3,1,0:T(8,128)(2,1)}, u32[]{:S(2)}) copy-start(bf16[1,4,128,1280]{2,3,1,0:T(8,128)(2,1)} %get-tuple-element.38) | copy-start | bytes 3932164
  106.3 116.2 %all-gather.10.cloned.1.call-start = ((), (), s32[]{:S(2)}) async-start(), calls=%async_computation.8 | async-start | bytes 1638400 | tf_op jit(solution)/shard_map/all_gather | solution.py:53
  134.5 20.3 %collective-permute-start.5 = (bf16[2,1,128,1280]{3,2,1,0:T(8,128)(2,1)}, bf16[2,1,128,1280]{3,2,1,0:T(8,128)(2,1)}, u32[]{:S(2)}, u32[]{:S(2)}) collective-permute-start(bf16[2,1,128,1280]{3,2,1,0:T(8,128)(2,1)} %copy.181), channel_id=1, source_target_pairs={{4,0},{8,4},{12,8},{16,12},{20,16},{24,20},{28,24},{32,28},{36,32}... | collective-permute-start | bytes 1966088 | tf_op jit(solution)/shard_map/ppermute | solution.py:17
  141.5 28.4 %collective-permute-start.4 = (bf16[2,1,128,1280]{3,2,1,0:T(8,128)(2,1)}, bf16[2,1,128,1280]{3,2,1,0:T(8,128)(2,1)}, u32[]{:S(2)}, u32[]{:S(2)}) collective-permute-start(bf16[2,1,128,1280]{3,2,1,0:T(8,128)(2,1)} %copy.180), channel_id=1, source_target_pairs={{0,4},{4,8},{8,12},{12,16},{16,20},{20,24},{24,28},{28,32},{32,36}... | collective-permute-start | bytes 1966088 | tf_op jit(solution)/shard_map/ppermute | solution.py:16
  176.7 5.0 %copy-start.20 = (bf16[4,128,320]{1,2,0:T(8,128)(2,1)S(1)}, bf16[4,128,320]{1,2,0:T(8,128)(2,1)}, u32[]{:S(2)}) copy-start(bf16[4,128,320]{1,2,0:T(8,128)(2,1)} %get-tuple-element.46) | copy-start | bytes 983044
  176.7 37.5 %all-to-all-start.2 = ((bf16[4,6,128,320]{2,3,1,0:T(8,128)(2,1)}), bf16[4,6,128,320]{2,3,1,0:T(8,128)(2,1)S(1)}, u32[]{:S(2)}, u32[]{:S(2)}) async-start(bf16[4,6,128,320]{2,3,1,0:T(8,128)(2,1)} %copy.184), calls=%async_computation.2 | async-start | bytes 3932160 | tf_op jit(solution)/shard_map/all_to_all | solution.py:51
  181.7 6.3 %collective-permute-start.3 = (bf16[1,128,320]{1,2,0:T(8,128)(2,1)S(1)}, bf16[1,128,320]{1,2,0:T(8,128)(2,1)S(1)}, u32[]{:S(2)}, u32[]{:S(2)}) collective-permute-start(bf16[1,128,320]{1,2,0:T(8,128)(2,1)S(1)} %get-tuple-element.51), channel_id=1, source_target_pairs={{4,0},{8,4},{12,8},{16,12},{20,16},{24,20},{28,24},{32,28},{36,32}... | collective-permute-start | bytes 245768 | tf_op jit(solution)/shard_map/ppermute | solution.py:17
  183.8 9.4 %collective-permute-start.2 = (bf16[1,128,320]{1,2,0:T(8,128)(2,1)S(1)}, bf16[1,128,320]{1,2,0:T(8,128)(2,1)S(1)}, u32[]{:S(2)}, u32[]{:S(2)}) collective-permute-start(bf16[1,128,320]{1,2,0:T(8,128)(2,1)S(1)} %get-tuple-element.50), channel_id=1, source_target_pairs={{0,4},{4,8},{8,12},{12,16},{16,20},{20,24},{24,28},{28,32},{32,36}... | collective-permute-start | bytes 245768 | tf_op jit(solution)/shard_map/ppermute | solution.py:16
  214.2 77.0 %all-to-all-start.1 = ((f32[4,4,128,320]{2,3,1,0:T(8,128)}), f32[4,4,128,320]{2,3,1,0:T(8,128)}, u32[]{:S(2)}, u32[]{:S(2)}) async-start(f32[4,4,128,320]{2,3,1,0:T(8,128)} %copy.178), calls=%async_computation.1 | async-start | bytes 5242880 | tf_op jit(solution)/shard_map/all_to_all | solution.py:43
  236.5 3.6 copy-start.14
  242.2 3.6 copy-start.12
  247.9 3.6 copy-start.10
  253.7 4.0 copy-start.8
  259.9 3.6 copy-start.6
  271.2 3.6 copy-start.2
  291.2 29.4 %all-to-all-start.4 = ((bf16[4,6,128,320]{2,3,1,0:T(8,128)(2,1)}), bf16[4,6,128,320]{2,3,1,0:T(8,128)(2,1)S(1)}, u32[]{:S(2)}, u32[]{:S(2)}) async-start(bf16[4,6,128,320]{2,3,1,0:T(8,128)(2,1)} %copy.198), calls=%async_computation.4 | async-start | bytes 3932160 | tf_op jit(solution)/shard_map/all_to_all | solution.py:51
  320.6 72.7 %all-to-all-start.3 = ((f32[8,9,40,320]{3,2,1,0:T(8,128)}), f32[8,9,40,320]{3,2,1,0:T(8,128)}, u32[]{:S(2)}, u32[]{:S(2)}) async-start(f32[8,9,40,320]{3,2,1,0:T(8,128)} %copy.197), calls=%async_computation.3 | async-start | bytes 8847360 | tf_op jit(solution)/shard_map/all_to_all | solution.py:43
  332.4 3.6 copy-start.15
  338.0 3.6 copy-start.13
  343.7 3.6 copy-start.11
  349.4 3.6 copy-start.9
  355.0 3.6 copy-start.7
  360.7 3.8 copy-start.5
  366.6 3.6 copy-start.3
  393.3 57.2 %all-to-all-start.5 = ((f32[8,9,40,320]{3,2,1,0:T(8,128)}), f32[8,9,40,320]{3,2,1,0:T(8,128)}, u32[]{:S(2)}, u32[]{:S(2)}) async-start(f32[8,9,40,320]{3,2,1,0:T(8,128)} %copy.209), calls=%async_computation.5 | async-start | bytes 8847360 | tf_op jit(solution)/shard_map/all_to_all | solution.py:43
  (25 other events, 42.3 us)
Sparse Core Ops, SparseCore 0:
  20.1 28.0 all-gather.5
  105.7 22.5 all-gather.7
  130.0 23.4 all-gather.11
  155.6 46.4 all-gather.9

commit v3 on v2

--- a/solution.py
+++ b/solution.py
@@ -51,20 +51,17 @@
     fields = lax.all_to_all(pieces, "ry", 0, 0, tiled=True)
     fields = jnp.pad(fields, ((0, 0), (0, 0), (1, 1), (0, 0)))
     grads_all = lax.all_gather(grads, "ry", axis=0, tiled=False)
-    flat_grads = grads_all.reshape(groups * rows * cols, out_width)
-    taps = []
-    for row_tap in range(3):
-        for col_tap in range(3):
-            window = fields[:, row_tap : row_tap + rows, col_tap : col_tap + cols]
-            window = window.reshape(groups * rows * cols, width)
-            taps.append(
-                lax.dot_general(
-                    window, flat_grads, (((0,), (0,)), ((), ())), preferred_element_type=jnp.float32
-                )
-            )
+    partial = lax.conv_general_dilated(
+        fields,
+        grads_all,
+        (1, 1),
+        "VALID",
+        dimension_numbers=("CHWN", "IHWO", "HWNC"),
+        preferred_element_type=jnp.float32,
+    )
     parts = lax.axis_size("rk")
-    partial = jnp.stack([t.reshape(parts, width // parts, out_width) for t in taps], axis=1)
-    return reduce_chunks(partial, "rk").reshape(3, 3, width // parts, out_width)
+    partial = partial.reshape(3, 3, parts, width // parts, out_width).transpose(2, 0, 1, 3, 4)
+    return reduce_chunks(partial, "rk")
 
 
 def make_body(groups, row_devices):

time: 470 us -> 424 us (0.902)
  local copies, waits for them, and re-layouts: 190 us -> 81.3 us
  waiting for transfers between devices: 116 us -> 180 us
    reshape x20 -> x2, local copies, waits for them, and re-layouts: 64.5 us -> 4.82 us  [weight_grad(): partial.reshape(3, 3, parts, width // parts, out_width)]
    all_to_all x4, waiting for transfers between devices: 53 us -> 101 us  [reduce_chunks(): received = lax.all_to_all(chunks, axis, 0, 0, tiled=True)]
    slice x20 -> x0, local copies, waits for them, and re-layouts: 45 us -> none  [weight_grad(): window = fields[:, row_tap:row_tap + rows, col_tap:col_tap + cols]]
    conv_general_dilated x0 -> x2, matrix products: none -> 28 us  [weight_grad(): lax.conv_general_dilated(fields, grads_all, (1, 1), 'VALID', dimension_nu...]
    dot_general x18 -> x0, matrix products: 26.8 us -> none  [weight_grad(): lax.dot_general(window, flat_grads, (((0,), (0,)), ((), ())), preferred_e...]
    all_to_all x2, waiting for transfers between devices: 12.1 us -> 25.5 us  [weight_grad(): fields = lax.all_to_all(pieces, 'ry', 0, 0, tiled=True)]
    all_to_all x0 -> x2, local copies, waits for them, and re-layouts: none -> 7.22 us  [weight_grad(): fields = lax.all_to_all(pieces, 'ry', 0, 0, tiled=True)]
    another operation x2 -> x0, local copies, waits for them, and re-layouts: 6.88 us -> none  [weight_grad(): jnp.stack([t.reshape(parts, width // parts, out_width) for t in taps], ax...]
  transfers between devices with their start and end apart: 16 -> 16, of which waited for: 10 -> 10; matrix products, arithmetic and copies ran while one was open for 52% -> 31% of each run, Pallas kernels for 0% -> 0%
where the time goes in v3:
time: 424 us; the launch traced here: 417 us
  waiting for transfers between devices  180 us (42%)
  local copies, waits for them, and re-layouts  81.3 us (19%)
  matrix products  62.9 us (15%)
  starting transfers between devices  51.4 us (12%)
  other arithmetic  24.9 us (6%)
  between operations  17.1 us (4%)
    all_to_all x4, waiting for transfers between devices, reduce_chunks(): received = lax.all_to_all(chunks, axis, 0, 0, tiled=True)  101 us
    conv_general_dilated x4, matrix products, conv_rows(): lax.conv_general_dilated(padded[None], kernel, (1, 1), ((0, 0), (1, 1)),...  34.9 us
    conv_general_dilated x2, matrix products, weight_grad(): lax.conv_general_dilated(fields, grads_all, (1, 1), 'VALID', dimension_nu...  28 us
    all_to_all x2, waiting for transfers between devices, weight_grad(): fields = lax.all_to_all(pieces, 'ry', 0, 0, tiled=True)  25.5 us
    all_gather x2, waiting for transfers between devices, gathered(): joined = lax.all_gather(joined, 'chan', axis=2, tiled=True)  22.7 us
    ppermute x3, waiting for transfers between devices, extended(): before = lax.ppermute(last, axis, up)  19.4 us
    all_to_all x4, starting transfers between devices, reduce_chunks(): received = lax.all_to_all(chunks, axis, 0, 0, tiled=True)  18.6 us
    conv_general_dilated x22, local copies, waits for them, and re-layouts, conv_rows(): lax.conv_general_dilated(padded[None], kernel, (1, 1), ((0, 0), (1, 1)),...  15.7 us
  transfers between devices with their start and end apart: 16, of which 10 were waited for; matrix products, arithmetic and copies ran while one was open for 31% of the time, Pallas kernels for 0%

profile of v3, /device:TPU:8, one launch (start us, length us, event | category | flops | bytes accessed | tf_op | source)
XLA Modules:
  0.0 417.3 jit_solution(9445034421708887438)
XLA Ops:
  9.0 6.8 %collective-permute-start.1 = (bf16[1,128,320]{1,2,0:T(8,128)(2,1)S(1)}, bf16[1,128,320]{1,2,0:T(8,128)(2,1)S(1)}, u32[]{:S(2)}, u32[]{:S(2)}) collective-permute-start(bf16[1,128,320]{1,2,0:T(8,128)(2,1)S(1)} %get-tuple-element.31), channel_id=1, source_target_pairs={{4,0},{8,4},{12,8},{16,12},{20,16},{24,20},{28,24},{32,28},{36,32}... | collective-permute-start | bytes 245768 | tf_op jit(solution)/shard_map/ppermute | solution.py:17
  20.8 4.3 %collective-permute-done = bf16[1,128,320]{1,2,0:T(8,128)(2,1)S(1)} collective-permute-done((bf16[1,128,320]{1,2,0:T(8,128)(2,1)S(1)}, bf16[1,128,320]{1,2,0:T(8,128)(2,1)S(1)}, u32[]{:S(2)}, u32[]{:S(2)}) %collective-permute-start) | collective-permute-done | bytes 81952 | tf_op jit(solution)/shard_map/ppermute | solution.py:16
  26.2 7.6 %convolution_select_fusion.1 = f32[4,8,17,1280]{3,1,2,0:T(8,128)S(1)} fusion(bf16[3,3,1280,320]{2,3,1,0:T(8,128)(2,1)} %param.12, pred[8,17]{0,1:T(8,128)(4,1)S(1)} %copy-done.12, bf16[6,1,7,2,320]{4,2,3,0,1:T(8,128)(2,1)S(1)} %slice.93, bf16[6,1,8,17,320]{4,2,3,0,1:T(8,128)(2,1)S(1)} %copy.65), kind=kOutput, calls=%fused_computation.7 | convolution fusion | flops 4013250560 | bytes 10734216 | tf_op jit(solution)/shard_map/conv_general_dilated | solution.py:27
  37.9 3.5 copy.68
  41.4 4.2 all-to-all-start
  47.9 30.4 %all-to-all-done = f32[4,4,128,320]{2,3,1,0:T(8,128)S(1)} async-done(((f32[4,4,128,320]{2,3,1,0:T(8,128)}), f32[4,4,128,320]{2,3,1,0:T(8,128)S(1)}, u32[]{:S(2)}, u32[]{:S(2)}) %all-to-all-start) | async-done | bytes 2621472 | tf_op jit(solution)/shard_map/all_to_all | solution.py:43
  85.7 3.4 pad.3.clone
  92.3 10.7 %add_multiply_fusion = (f32[4,8,17,320]{3,1,2,0:T(8,128)}, f32[4,8,17,320]{3,1,2,0:T(8,128)S(1)}) fusion(f32[320]{0:T(512)S(1)} %select_reduce_fusion, bf16[3,3,1280,320]{2,3,1,0:T(8,128)(2,1)} %param.11, bf16[6,1,7,2,1280]{4,2,3,0,1:T(8,128)(2,1)S(1)} %slice.86, bf16[6,1,8,17,1280]{4,2,3,0,1:T(8,128)(2,1)S(1)} %copy.55, pred[8,17]{0,1:T(8,128)(4,1)S(1)} %copy-done.12), kind=kOutput, calls=%fused_computation.35 | convolution fusion | flops 4019374080 | bytes 11070856 | tf_op jit(solution)/shard_map/conv_general_dilated | solution.py:27
  106.2 22.7 %all-gather.8.cloned.1.call-done = bf16[6,128,1280]{1,2,0:T(8,128)(2,1)} async-done(((bf16[6,128,320]{1,2,0:T(8,128)(2,1)}), bf16[6,128,1280]{1,2,0:T(8,128)(2,1)}) %all-gather.8.cloned.1.call-update) | async-done | bytes 1966096 | tf_op jit(solution)/shard_map/all_gather | solution.py:85
  134.9 4.8 %collective-permute-start.5 = (bf16[2,1,128,1280]{3,2,1,0:T(8,128)(2,1)}, bf16[2,1,128,1280]{3,2,1,0:T(8,128)(2,1)}, u32[]{:S(2)}, u32[]{:S(2)}) collective-permute-start(bf16[2,1,128,1280]{3,2,1,0:T(8,128)(2,1)} %copy.78), channel_id=1, source_target_pairs={{4,0},{8,4},{12,8},{16,12},{20,16},{24,20},{28,24},{32,28},{36,32}... | collective-permute-start | bytes 1966088 | tf_op jit(solution)/shard_map/ppermute | solution.py:17
  144.3 10.9 %collective-permute-done.5 = bf16[2,1,128,1280]{3,2,1,0:T(8,128)(2,1)} collective-permute-done((bf16[2,1,128,1280]{3,2,1,0:T(8,128)(2,1)}, bf16[2,1,128,1280]{3,2,1,0:T(8,128)(2,1)}, u32[]{:S(2)}, u32[]{:S(2)}) %collective-permute-start.5) | collective-permute-done | bytes 655392 | tf_op jit(solution)/shard_map/ppermute | solution.py:17
  157.3 13.1 %collective-permute-done.4 = bf16[2,1,128,1280]{3,2,1,0:T(8,128)(2,1)} collective-permute-done((bf16[2,1,128,1280]{3,2,1,0:T(8,128)(2,1)}, bf16[2,1,128,1280]{3,2,1,0:T(8,128)(2,1)}, u32[]{:S(2)}, u32[]{:S(2)}) %collective-permute-start.4) | collective-permute-done | bytes 655392 | tf_op jit(solution)/shard_map/ppermute | solution.py:16
  177.4 4.8 %all-to-all-start.2 = ((bf16[4,6,128,320]{2,3,1,0:T(8,128)(2,1)}), bf16[4,6,128,320]{2,3,1,0:T(8,128)(2,1)S(1)}, u32[]{:S(2)}, u32[]{:S(2)}) async-start(bf16[4,6,128,320]{2,3,1,0:T(8,128)(2,1)} %copy.81), calls=%async_computation.2 | async-start | bytes 3932160 | tf_op jit(solution)/shard_map/all_to_all | solution.py:51
  189.9 25.5 %all-to-all-done.2 = bf16[4,6,128,320]{2,3,1,0:T(8,128)(2,1)S(1)} async-done(((bf16[4,6,128,320]{2,3,1,0:T(8,128)(2,1)}), bf16[4,6,128,320]{2,3,1,0:T(8,128)(2,1)S(1)}, u32[]{:S(2)}, u32[]{:S(2)}) %all-to-all-start.2) | async-done | bytes 1966112 | tf_op jit(solution)/shard_map/all_to_all | solution.py:51
  215.4 6.0 %all-to-all-start.4 = ((bf16[4,6,128,320]{2,3,1,0:T(8,128)(2,1)}), bf16[4,6,128,320]{2,3,1,0:T(8,128)(2,1)}, u32[]{:S(2)}, u32[]{:S(2)}) async-start(bf16[4,6,128,320]{2,3,1,0:T(8,128)(2,1)} %copy.87), calls=%async_computation.4 | async-start | bytes 3932160 | tf_op jit(solution)/shard_map/all_to_all | solution.py:51
  223.4 3.9 collective-permute-start.2
  227.4 3.6 copy.89
  233.8 7.6 %convolution_select_fusion = f32[4,8,17,1280]{3,1,2,0:T(8,128)S(1)} fusion(bf16[3,3,1280,320]{2,3,1,0:T(8,128)(2,1)} %param.11, pred[8,17]{0,1:T(8,128)(4,1)S(1)} %copy-done.12, bf16[6,1,7,2,320]{4,2,3,0,1:T(8,128)(2,1)S(1)} %slice.97, bf16[6,1,8,17,320]{4,2,3,0,1:T(8,128)(2,1)S(1)} %copy.72), kind=kOutput, calls=%fused_computation.6 | convolution fusion | flops 4013250560 | bytes 10734216 | tf_op jit(solution)/shard_map/conv_general_dilated | solution.py:27
  245.4 3.5 copy.75
  248.9 3.7 copy.85
  252.5 3.2 copy.84
  255.8 4.9 %all-to-all-start.1 = ((f32[4,4,128,320]{2,3,1,0:T(8,128)}), f32[4,4,128,320]{2,3,1,0:T(8,128)}, u32[]{:S(2)}, u32[]{:S(2)}) async-start(f32[4,4,128,320]{2,3,1,0:T(8,128)} %copy.75), calls=%async_computation.1 | async-start | bytes 5242880 | tf_op jit(solution)/shard_map/all_to_all | solution.py:43
  260.6 14.0 %fusion.74 = f32[3,3,320,320]{3,2,1,0:T(8,128)S(1)} fusion(bf16[4,6,128,320]{3,0,2,1:T(4,128)(2,1)S(1)} %copy-done.8, bf16[4,4,128,320]{3,0,2,1:T(4,128)(2,1)} %copy.85), kind=kOutput, calls=%fused_computation.104 | convolution fusion | flops 3755212800 | bytes 6963200 | tf_op jit(solution)/shard_map/conv_general_dilated | solution.py:54
  277.1 4.0 copy.88
  281.1 12.4 %all-to-all-done.1 = f32[4,4,128,320]{2,3,1,0:T(8,128)} async-done(((f32[4,4,128,320]{2,3,1,0:T(8,128)}), f32[4,4,128,320]{2,3,1,0:T(8,128)}, u32[]{:S(2)}, u32[]{:S(2)}) %all-to-all-start.1) | async-done | bytes 2621472 | tf_op jit(solution)/shard_map/all_to_all | solution.py:43
  293.5 4.8 %all-to-all-start.3 = ((f32[8,3,3,40,320]{4,3,2,1,0:T(8,128)}), f32[8,3,3,40,320]{4,3,2,1,0:T(8,128)}, u32[]{:S(2)}, u32[]{:S(2)}) async-start(f32[8,3,3,40,320]{4,3,2,1,0:T(8,128)} %bitcast.99), calls=%async_computation.3 | async-start | bytes 8847360 | tf_op jit(solution)/shard_map/all_to_all | solution.py:43
  298.3 14.0 %fusion.75 = f32[3,3,320,320]{3,2,1,0:T(8,128)S(1)} fusion(bf16[4,6,128,320]{3,0,2,1:T(4,128)(2,1)S(1)} %copy.88, bf16[4,4,128,320]{3,0,2,1:T(4,128)(2,1)} %copy.89), kind=kOutput, calls=%fused_computation.105 | convolution fusion | flops 3755212800 | bytes 6963200 | tf_op jit(solution)/shard_map/conv_general_dilated | solution.py:54
  314.6 35.5 %all-to-all-done.3 = f32[8,3,3,40,320]{4,3,2,1,0:T(8,128)} async-done(((f32[8,3,3,40,320]{4,3,2,1,0:T(8,128)}), f32[8,3,3,40,320]{4,3,2,1,0:T(8,128)}, u32[]{:S(2)}, u32[]{:S(2)}) %all-to-all-start.3) | async-done | bytes 3686432 | tf_op jit(solution)/shard_map/all_to_all | solution.py:43
  350.1 4.8 %all-to-all-start.5 = ((f32[8,3,3,40,320]{4,3,2,1,0:T(8,128)}), f32[8,3,3,40,320]{4,3,2,1,0:T(8,128)}, u32[]{:S(2)}, u32[]{:S(2)}) async-start(f32[8,3,3,40,320]{4,3,2,1,0:T(8,128)} %bitcast.98), calls=%async_computation.5 | async-start | bytes 8847360 | tf_op jit(solution)/shard_map/all_to_all | solution.py:43
  361.6 3.3 pad.5.clone
  368.3 9.0 %fusion.18 = f32[4,8,17,320]{3,1,2,0:T(8,128)S(1)} fusion(bf16[3,3,1280,320]{2,3,1,0:T(8,128)(2,1)} %param.12, bf16[6,1,7,2,1280]{4,2,3,0,1:T(8,128)(2,1)S(1)} %slice.91, bf16[6,1,8,17,1280]{4,2,3,0,1:T(8,128)(2,1)S(1)} %copy.60, pred[8,17]{0,1:T(8,128)(4,1)S(1)} %copy-done.13), kind=kOutput, calls=%fused_computation.31 | convolution fusion | flops 4017981440 | bytes 10373256 | tf_op jit(solution)/shard_map/conv_general_dilated | solution.py:27
  383.2 22.8 %all-to-all-done.5 = f32[8,3,3,40,320]{4,3,2,1,0:T(8,128)} async-done(((f32[8,3,3,40,320]{4,3,2,1,0:T(8,128)}), f32[8,3,3,40,320]{4,3,2,1,0:T(8,128)}, u32[]{:S(2)}, u32[]{:S(2)}) %all-to-all-start.5) | async-done | bytes 3686432 | tf_op jit(solution)/shard_map/all_to_all | solution.py:43
  (117 shorter events, 86.6 us)
Async XLA Ops:
  8.0 17.2 %copy-start.5 = (bf16[4,128,320]{1,2,0:T(8,128)(2,1)S(1)}, bf16[4,128,320]{1,2,0:T(8,128)(2,1)}, u32[]{:S(2)}) copy-start(bf16[4,128,320]{1,2,0:T(8,128)(2,1)} %param.15) | copy-start | bytes 983044
  8.0 71.3 %all-gather.6.cloned.1.call-start = ((), (), s32[]{:S(2)}) async-start(), calls=%async_computation.6 | async-start | bytes 2457600 | tf_op jit(solution)/shard_map/all_gather | solution.py:85
  9.0 11.8 %collective-permute-start.1 = (bf16[1,128,320]{1,2,0:T(8,128)(2,1)S(1)}, bf16[1,128,320]{1,2,0:T(8,128)(2,1)S(1)}, u32[]{:S(2)}, u32[]{:S(2)}) collective-permute-start(bf16[1,128,320]{1,2,0:T(8,128)(2,1)S(1)} %get-tuple-element.31), channel_id=1, source_target_pairs={{4,0},{8,4},{12,8},{16,12},{20,16},{24,20},{28,24},{32,28},{36,32}... | collective-permute-start | bytes 245768 | tf_op jit(solution)/shard_map/ppermute | solution.py:17
  15.8 9.3 %collective-permute-start = (bf16[1,128,320]{1,2,0:T(8,128)(2,1)S(1)}, bf16[1,128,320]{1,2,0:T(8,128)(2,1)S(1)}, u32[]{:S(2)}, u32[]{:S(2)}) collective-permute-start(bf16[1,128,320]{1,2,0:T(8,128)(2,1)S(1)} %get-tuple-element.30), channel_id=1, source_target_pairs={{0,4},{4,8},{8,12},{12,16},{16,20},{20,24},{24,28},{28,32},{32,36}... | collective-permute-start | bytes 245768 | tf_op jit(solution)/shard_map/ppermute | solution.py:16
  25.5 0.7 copy-start.12
  41.4 6.5 %copy-start.11 = (bf16[2,128,320]{1,2,0:T(8,128)(2,1)S(1)}, bf16[2,128,320]{1,2,0:T(8,128)(2,1)}, u32[]{:S(2)}) copy-start(bf16[2,128,320]{1,2,0:T(8,128)(2,1)} %param.10) | copy-start | bytes 491524
  41.4 36.9 %all-to-all-start = ((f32[4,4,128,320]{2,3,1,0:T(8,128)}), f32[4,4,128,320]{2,3,1,0:T(8,128)S(1)}, u32[]{:S(2)}, u32[]{:S(2)}) async-start(f32[4,4,128,320]{2,3,1,0:T(8,128)} %copy.68), calls=%async_computation | async-start | bytes 5242880 | tf_op jit(solution)/shard_map/all_to_all | solution.py:43
  45.5 83.3 %all-gather.8.cloned.1.call-start = ((), (), s32[]{:S(2)}) async-start(), calls=%async_computation.7 | async-start | bytes 2457600 | tf_op jit(solution)/shard_map/all_gather | solution.py:85
  103.0 1.1 copy-start.3
  106.1 25.5 %copy-start = (bf16[1,4,128,1280]{2,3,1,0:T(8,128)(2,1)S(1)}, bf16[1,4,128,1280]{2,3,1,0:T(8,128)(2,1)}, u32[]{:S(2)}) copy-start(bf16[1,4,128,1280]{2,3,1,0:T(8,128)(2,1)} %get-tuple-element.16) | copy-start | bytes 3932164
  106.1 121.3 %all-gather.12.cloned.1.call-start = ((), (), s32[]{:S(2)}) async-start(), calls=%async_computation.9 | async-start | bytes 1638400 | tf_op jit(solution)/shard_map/all_gather | solution.py:53
  134.9 20.3 %collective-permute-start.5 = (bf16[2,1,128,1280]{3,2,1,0:T(8,128)(2,1)}, bf16[2,1,128,1280]{3,2,1,0:T(8,128)(2,1)}, u32[]{:S(2)}, u32[]{:S(2)}) collective-permute-start(bf16[2,1,128,1280]{3,2,1,0:T(8,128)(2,1)} %copy.78), channel_id=1, source_target_pairs={{4,0},{8,4},{12,8},{16,12},{20,16},{24,20},{28,24},{32,28},{36,32}... | collective-permute-start | bytes 1966088 | tf_op jit(solution)/shard_map/ppermute | solution.py:17
  141.9 28.6 %collective-permute-start.4 = (bf16[2,1,128,1280]{3,2,1,0:T(8,128)(2,1)}, bf16[2,1,128,1280]{3,2,1,0:T(8,128)(2,1)}, u32[]{:S(2)}, u32[]{:S(2)}) collective-permute-start(bf16[2,1,128,1280]{3,2,1,0:T(8,128)(2,1)} %copy.77), channel_id=1, source_target_pairs={{0,4},{4,8},{8,12},{12,16},{16,20},{20,24},{24,28},{28,32},{32,36}... | collective-permute-start | bytes 1966088 | tf_op jit(solution)/shard_map/ppermute | solution.py:16
  177.4 38.0 %all-to-all-start.2 = ((bf16[4,6,128,320]{2,3,1,0:T(8,128)(2,1)}), bf16[4,6,128,320]{2,3,1,0:T(8,128)(2,1)S(1)}, u32[]{:S(2)}, u32[]{:S(2)}) async-start(bf16[4,6,128,320]{2,3,1,0:T(8,128)(2,1)} %copy.81), calls=%async_computation.2 | async-start | bytes 3932160 | tf_op jit(solution)/shard_map/all_to_all | solution.py:51
  182.2 66.6 %all-gather.10.cloned.1.call-start = ((), (), s32[]{:S(2)}) async-start(), calls=%async_computation.8 | async-start | bytes 1638400 | tf_op jit(solution)/shard_map/all_gather | solution.py:53
  189.9 31.5 %copy-start.9 = (bf16[4,128,320]{1,2,0:T(8,128)(2,1)S(1)}, bf16[4,128,320]{1,2,0:T(8,128)(2,1)}, u32[]{:S(2)}) copy-start(bf16[4,128,320]{1,2,0:T(8,128)(2,1)} %get-tuple-element.24) | copy-start | bytes 983044
  215.4 15.5 %copy-start.1 = (bf16[4,6,128,320]{2,3,1,0:T(8,128)(2,1)}, bf16[4,6,128,320]{2,3,1,0:T(8,128)(2,1)S(1)}, u32[]{:S(2)}) copy-start(bf16[4,6,128,320]{2,3,1,0:T(8,128)(2,1)S(1)} %all-to-all-done.2) | copy-start | bytes 5898244
  215.4 40.3 %all-to-all-start.4 = ((bf16[4,6,128,320]{2,3,1,0:T(8,128)(2,1)}), bf16[4,6,128,320]{2,3,1,0:T(8,128)(2,1)}, u32[]{:S(2)}, u32[]{:S(2)}) async-start(bf16[4,6,128,320]{2,3,1,0:T(8,128)(2,1)} %copy.87), calls=%async_computation.4 | async-start | bytes 3932160 | tf_op jit(solution)/shard_map/all_to_all | solution.py:51
  221.5 9.5 %collective-permute-start.3 = (bf16[1,128,320]{1,2,0:T(8,128)(2,1)S(1)}, bf16[1,128,320]{1,2,0:T(8,128)(2,1)S(1)}, u32[]{:S(2)}, u32[]{:S(2)}) collective-permute-start(bf16[1,128,320]{1,2,0:T(8,128)(2,1)S(1)} %get-tuple-element.29), channel_id=1, source_target_pairs={{4,0},{8,4},{12,8},{16,12},{20,16},{24,20},{28,24},{32,28},{36,32}... | collective-permute-start | bytes 245768 | tf_op jit(solution)/shard_map/ppermute | solution.py:17
  223.4 9.4 %collective-permute-start.2 = (bf16[1,128,320]{1,2,0:T(8,128)(2,1)S(1)}, bf16[1,128,320]{1,2,0:T(8,128)(2,1)S(1)}, u32[]{:S(2)}, u32[]{:S(2)}) collective-permute-start(bf16[1,128,320]{1,2,0:T(8,128)(2,1)S(1)} %get-tuple-element.28), channel_id=1, source_target_pairs={{0,4},{4,8},{8,12},{12,16},{16,20},{20,24},{24,28},{28,32},{32,36}... | collective-permute-start | bytes 245768 | tf_op jit(solution)/shard_map/ppermute | solution.py:16
  248.8 3.7 copy-start.2
  255.8 4.9 %copy-start.8 = (bf16[4,6,128,320]{3,0,2,1:T(4,128)(2,1)S(1)}, bf16[4,6,128,320]{3,0,2,1:T(4,128)(2,1)}, u32[]{:S(2)}) copy-start(bf16[4,6,128,320]{3,0,2,1:T(4,128)(2,1)} %copy.84) | copy-start | bytes 5898244
  255.8 37.7 %all-to-all-start.1 = ((f32[4,4,128,320]{2,3,1,0:T(8,128)}), f32[4,4,128,320]{2,3,1,0:T(8,128)}, u32[]{:S(2)}, u32[]{:S(2)}) async-start(f32[4,4,128,320]{2,3,1,0:T(8,128)} %copy.75), calls=%async_computation.1 | async-start | bytes 5242880 | tf_op jit(solution)/shard_map/all_to_all | solution.py:43
  293.5 56.7 %all-to-all-start.3 = ((f32[8,3,3,40,320]{4,3,2,1,0:T(8,128)}), f32[8,3,3,40,320]{4,3,2,1,0:T(8,128)}, u32[]{:S(2)}, u32[]{:S(2)}) async-start(f32[8,3,3,40,320]{4,3,2,1,0:T(8,128)} %bitcast.99), calls=%async_computation.3 | async-start | bytes 8847360 | tf_op jit(solution)/shard_map/all_to_all | solution.py:43
  350.1 55.9 %all-to-all-start.5 = ((f32[8,3,3,40,320]{4,3,2,1,0:T(8,128)}), f32[8,3,3,40,320]{4,3,2,1,0:T(8,128)}, u32[]{:S(2)}, u32[]{:S(2)}) async-start(f32[8,3,3,40,320]{4,3,2,1,0:T(8,128)} %bitcast.98), calls=%async_computation.5 | async-start | bytes 8847360 | tf_op jit(solution)/shard_map/all_to_all | solution.py:43
  355.0 4.0 copy-start.4
  367.6 0.7 copy-start.13
  377.4 1.0 copy-start.6
  377.4 1.2 copy-start.7
  377.4 1.3 copy-start.10
Sparse Core Ops, SparseCore 0:
  20.9 28.0 all-gather.5
  106.2 22.5 all-gather.7
Sparse Core Ops, SparseCore 1:
  144.3 25.3 all-gather.11
  186.9 28.8 all-gather.9
